TPU v7x, 128 devices: a whole 4x4x4 slice. The times are simulated.
128 devices in a mesh: month: 4 (over x), grid: 32 (over y, z, core).
Axes of the slice: x: 4, y: 4, z: 4, core: 2. Of those that a mesh axis runs over, the one named last changes fastest.
Arguments:
- tracers: float32 [64, 32768], P(None, 'grid'), may hold values from 0.25 to 7
- targets: float32 [64], replicated, may hold values from 0.5 to 2
- retain: float32 [8, 32768], P('month', 'grid'), may hold values from 0.5 to 0.95
- blocks: float32 [8, 256, 8, 128, 128], P('month', 'grid'), may hold values from 3.90625e-07 to 0.00390625
- cols: int32 [8, 256, 8], P('month', 'grid'), may hold values from 0 to 255, as said below
Outputs:
- spun_up: float32 [64, 32768], P('month', 'grid')
Inputs may be any that keep to these rules, and one draw needn't show every extreme that they name: cols[m, i, 0] = i; for 1 <= k < 6, cols[m, i, k] names a block on the same grid device as block i (block b lies on device b // 8); the last 2 entries name blocks on other devices, and of the 16 such entries of one device's block rows in one month at most 1 lie on any single device, exactly 1 on some.
All inputs are finite; a program needn't handle non-finite values.
Results may differ from a plain program's by a relative error of at most 0.0001.
Values sent between devices are 32-bit elements; how exact they have to be, the bound alone decides.
No kernel may reach another device: no remote copies, remote signals or barrier semaphores. Data moves between devices by JAX's collectives and lax.ppermute only.
A program may use at most 64 MiB of HBM per device.

v0:
```python
import jax
import jax.numpy as jnp
from jax import lax
from jax.sharding import PartitionSpec as P


def passed_along(value, axis, by):
    devices = lax.axis_size(axis)
    return lax.ppermute(value, axis, [(i, (i + by) % devices) for i in range(devices)])


def local(tracers, targets, retain, blocks, cols):
    sections = lax.axis_size("month")
    devices = lax.axis_size("grid")
    section = lax.axis_index("month")
    months_here = blocks.shape[0]
    blk_count = blocks.shape[1]
    blk_size = blocks.shape[3]
    rows_here = blk_count * blk_size
    batch = tracers.shape[0] // sections
    points = rows_here * devices
    held = jnp.zeros((batch, rows_here), jnp.float32)
    kept = jnp.zeros((batch, rows_here), jnp.float32)
    last_step = max(2 * sections - 2, 3 * sections - 4)
    for step in range(last_step + 1):
        if step < sections:
            held = jnp.where(section == 0, tracers[step * batch : (step + 1) * batch], held)
        if step < 2 * sections - 1:
            working = (step - section >= 0) & (step - section < sections)
            apply_state = held
            for apply_month_idx in range(months_here):
                whole = lax.all_gather(apply_state, "grid", axis=1, tiled=True)
                picked = whole.reshape(batch, -1, blk_size)[:, cols[apply_month_idx]]
                mixed = jnp.einsum(
                    "tbkc,bkrc->tbr",
                    picked,
                    blocks[apply_month_idx],
                    precision=lax.Precision.HIGHEST,
                    preferred_element_type=jnp.float32,
                )
                apply_state = retain[apply_month_idx][None, :] * apply_state + mixed.reshape(
                    batch, rows_here
                )
            held = jnp.where(working, apply_state, held)
            finished = step - sections + 1
            if finished >= 0:
                inventory = lax.psum(jnp.sum(held, axis=1), "grid")
                goal = targets[finished * batch : (finished + 1) * batch]
                scaled = held * (goal * points / inventory)[:, None]
                held = jnp.where(section == sections - 1, scaled, held)
        arrived = jnp.where(
            section == sections - 1, step == 2 * sections - 2, step == sections + 2 * section
        )
        kept = jnp.where(arrived, held, kept)
        if step < last_step:
            held = passed_along(held, "month", 1)
    return kept


def solution(mesh):
    return jax.shard_map(
        local,
        mesh=mesh,
        in_specs=(
            P(None, "grid"),
            P(),
            P("month", "grid"),
            P("month", "grid", None, None, None),
            P("month", "grid", None),
        ),
        out_specs=P("month", "grid"),
        check_vma=False,
    )
```

profile of v0, /device:TPU:0, one launch (start us, length us, event | category | flops | bytes accessed | tf_op | source)
XLA Modules:
  0.0 1031.2 jit_solution(10049208585597531722)
XLA Ops:
  6.5 1.5 slice_select_fusion
  8.9 0.8 fusion.99
  9.7 46.3 %all-gather.15.cloned.1.call-done = f32[16,32768]{1,0:T(8,128)} async-done(((f32[16,1024]{1,0:T(8,128)}), f32[16,32768]{1,0:T(8,128)}) %all-gather.15.cloned.1.call-update) | async-done | bytes 2097168 | tf_op jit(solution)/shard_map/all_gather | solution.py:32
  56.0 1.7 copy_bitcast_fusion.13
  58.4 5.3 fusion.42
  64.6 43.0 %all-gather.17.cloned.1.call-done = f32[16,32768]{1,0:T(8,128)} async-done(((f32[16,1024]{1,0:T(8,128)}), f32[16,32768]{1,0:T(8,128)}) %all-gather.17.cloned.1.call-update) | async-done | bytes 2097168 | tf_op jit(solution)/shard_map/all_gather | solution.py:32
  107.6 1.7 copy_bitcast_fusion.12
  110.0 5.3 fusion.63
  115.4 1.5 collective-permute-start
  116.9 4.0 collective-permute-done
  121.6 41.9 %all-gather.19.cloned.1.call-done = f32[16,32768]{1,0:T(8,128)} async-done(((f32[16,1024]{1,0:T(8,128)}), f32[16,32768]{1,0:T(8,128)}) %all-gather.19.cloned.1.call-update) | async-done | bytes 2097168 | tf_op jit(solution)/shard_map/all_gather | solution.py:32
  163.5 1.7 copy_bitcast_fusion.11
  166.0 5.3 fusion.45
  172.0 43.1 %all-gather.21.cloned.1.call-done = f32[16,32768]{1,0:T(8,128)} async-done(((f32[16,1024]{1,0:T(8,128)}), f32[16,32768]{1,0:T(8,128)}) %all-gather.21.cloned.1.call-update) | async-done | bytes 2097168 | tf_op jit(solution)/shard_map/all_gather | solution.py:32
  215.1 1.7 copy_bitcast_fusion.10
  217.5 5.3 fusion.66
  222.9 1.5 collective-permute-start.1
  224.4 4.0 collective-permute-done.1
  229.2 41.9 %all-gather.23.cloned.1.call-done = f32[16,32768]{1,0:T(8,128)} async-done(((f32[16,1024]{1,0:T(8,128)}), f32[16,32768]{1,0:T(8,128)}) %all-gather.23.cloned.1.call-update) | async-done | bytes 2097168 | tf_op jit(solution)/shard_map/all_gather | solution.py:32
  271.1 1.7 copy_bitcast_fusion.9
  273.5 5.3 fusion.48
  279.7 42.9 %all-gather.25.cloned.1.call-done = f32[16,32768]{1,0:T(8,128)} async-done(((f32[16,1024]{1,0:T(8,128)}), f32[16,32768]{1,0:T(8,128)}) %all-gather.25.cloned.1.call-update) | async-done | bytes 2097168 | tf_op jit(solution)/shard_map/all_gather | solution.py:32
  322.7 1.7 copy_bitcast_fusion.8
  325.1 5.3 fusion.69
  330.4 1.5 collective-permute-start.2
  332.0 4.0 collective-permute-done.2
  336.7 41.9 %all-gather.27.cloned.1.call-done = f32[16,32768]{1,0:T(8,128)} async-done(((f32[16,1024]{1,0:T(8,128)}), f32[16,32768]{1,0:T(8,128)}) %all-gather.27.cloned.1.call-update) | async-done | bytes 2097168 | tf_op jit(solution)/shard_map/all_gather | solution.py:32
  378.6 1.7 copy_bitcast_fusion.7
  381.0 5.3 fusion.51
  387.1 43.1 %all-gather.29.cloned.1.call-done = f32[16,32768]{1,0:T(8,128)} async-done(((f32[16,1024]{1,0:T(8,128)}), f32[16,32768]{1,0:T(8,128)}) %all-gather.29.cloned.1.call-update) | async-done | bytes 2097168 | tf_op jit(solution)/shard_map/all_gather | solution.py:32
  430.2 1.7 copy_bitcast_fusion.6
  432.6 5.3 fusion.72
  438.1 65.2 %psum.28 = f32[16]{0:T(128)S(1)} all-reduce(f32[16]{0:T(128)S(1)} %get-tuple-element.11), channel_id=1, replica_groups=mesh['month'=4,'grid'=32] {'grid'}, use_global_device_ids=true, to_apply=%region_1.2 | all-reduce | flops 16 | bytes 128 | tf_op jit(solution)/shard_map/psum | solution.py:47
  503.3 1.5 collective-permute-start.3
  504.8 4.0 collective-permute-done.3
  509.5 38.9 %all-gather.31.cloned.1.call-done = f32[16,32768]{1,0:T(8,128)} async-done(((f32[16,1024]{1,0:T(8,128)}), f32[16,32768]{1,0:T(8,128)}) %all-gather.31.cloned.1.call-update) | async-done | bytes 2097168 | tf_op jit(solution)/shard_map/all_gather | solution.py:32
  548.4 1.7 copy_bitcast_fusion.5
  550.8 5.3 fusion.54
  556.9 43.1 %all-gather.33.cloned.1.call-done = f32[16,32768]{1,0:T(8,128)} async-done(((f32[16,1024]{1,0:T(8,128)}), f32[16,32768]{1,0:T(8,128)}) %all-gather.33.cloned.1.call-update) | async-done | bytes 2097168 | tf_op jit(solution)/shard_map/all_gather | solution.py:32
  600.0 1.7 copy_bitcast_fusion.4
  602.4 5.3 fusion.75
  607.9 65.2 %psum.29 = f32[16]{0:T(128)S(1)} all-reduce(f32[16]{0:T(128)S(1)} %get-tuple-element.9), channel_id=1, replica_groups=mesh['month'=4,'grid'=32] {'grid'}, use_global_device_ids=true, to_apply=%region_3.4 | all-reduce | flops 16 | bytes 128 | tf_op jit(solution)/shard_map/psum | solution.py:47
  673.2 1.5 collective-permute-start.4
  674.7 4.0 collective-permute-done.4
  679.6 38.7 %all-gather.35.cloned.1.call-done = f32[16,32768]{1,0:T(8,128)} async-done(((f32[16,1024]{1,0:T(8,128)}), f32[16,32768]{1,0:T(8,128)}) %all-gather.35.cloned.1.call-update) | async-done | bytes 2097168 | tf_op jit(solution)/shard_map/all_gather | solution.py:32
  718.3 1.7 copy_bitcast_fusion.3
  720.7 5.3 fusion.57
  726.8 43.1 %all-gather.37.cloned.1.call-done = f32[16,32768]{1,0:T(8,128)} async-done(((f32[16,1024]{1,0:T(8,128)}), f32[16,32768]{1,0:T(8,128)}) %all-gather.37.cloned.1.call-update) | async-done | bytes 2097168 | tf_op jit(solution)/shard_map/all_gather | solution.py:32
  769.9 1.7 copy_bitcast_fusion.2
  772.3 5.3 fusion.78
  777.8 65.2 %psum.30 = f32[16]{0:T(128)S(1)} all-reduce(f32[16]{0:T(128)S(1)} %get-tuple-element.7), channel_id=1, replica_groups=mesh['month'=4,'grid'=32] {'grid'}, use_global_device_ids=true, to_apply=%region_5.6 | all-reduce | flops 16 | bytes 128 | tf_op jit(solution)/shard_map/psum | solution.py:47
  843.1 1.5 collective-permute-start.5
  844.6 4.0 collective-permute-done.5
  849.3 38.9 %all-gather.39.cloned.1.call-done = f32[16,32768]{1,0:T(8,128)} async-done(((f32[16,1024]{1,0:T(8,128)}), f32[16,32768]{1,0:T(8,128)}) %all-gather.39.cloned.1.call-update) | async-done | bytes 2097168 | tf_op jit(solution)/shard_map/all_gather | solution.py:32
  888.2 1.7 copy_bitcast_fusion.1
  890.6 5.3 fusion.60
  896.6 43.2 %all-gather.41.cloned.1.call-done = f32[16,32768]{1,0:T(8,128)} async-done(((f32[16,1024]{1,0:T(8,128)}), f32[16,32768]{1,0:T(8,128)}) %all-gather.41.cloned.1.call-update) | async-done | bytes 2097168 | tf_op jit(solution)/shard_map/all_gather | solution.py:32
  939.8 1.7 copy_bitcast_fusion
  942.2 5.3 fusion.81
  947.6 65.2 %psum.31 = f32[16]{0:T(128)S(1)} all-reduce(f32[16]{0:T(128)S(1)} %get-tuple-element.5), channel_id=1, replica_groups=mesh['month'=4,'grid'=32] {'grid'}, use_global_device_ids=true, to_apply=%region_7.8 | all-reduce | flops 16 | bytes 128 | tf_op jit(solution)/shard_map/psum | solution.py:47
  1013.0 1.5 collective-permute-start.6
  1014.4 4.0 collective-permute-done.6
  1019.0 5.0 collective-permute-done.7
  1023.9 0.7 select_select_fusion
  (109 shorter events, 21.1 us)
Async XLA Ops:
  6.5 49.5 %all-gather.15.cloned.1.call-start = ((), (), s32[]{:S(2)}) async-start(), calls=%async_computation | async-start | bytes 2162688 | tf_op jit(solution)/shard_map/all_gather | solution.py:32
  8.0 99.6 %all-gather.17.cloned.1.call-start = ((), (), s32[]{:S(2)}) async-start(), calls=%async_computation.1 | async-start | bytes 2162688 | tf_op jit(solution)/shard_map/all_gather | solution.py:32
  58.4 5.3 copy-start.3
  64.4 99.1 %all-gather.19.cloned.1.call-start = ((), (), s32[]{:S(2)}) async-start(), calls=%async_computation.2 | async-start | bytes 2162688 | tf_op jit(solution)/shard_map/all_gather | solution.py:32
  110.0 5.3 copy-start.10
  115.4 5.5 collective-permute-start
  121.6 93.6 %all-gather.21.cloned.1.call-start = ((), (), s32[]{:S(2)}) async-start(), calls=%async_computation.3 | async-start | bytes 2162688 | tf_op jit(solution)/shard_map/all_gather | solution.py:32
  165.9 5.3 copy-start.1
  172.0 99.1 %all-gather.23.cloned.1.call-start = ((), (), s32[]{:S(2)}) async-start(), calls=%async_computation.4 | async-start | bytes 2162688 | tf_op jit(solution)/shard_map/all_gather | solution.py:32
  217.5 5.3 copy-start.15
  222.9 5.5 collective-permute-start.1
  229.1 93.6 %all-gather.25.cloned.1.call-start = ((), (), s32[]{:S(2)}) async-start(), calls=%async_computation.5 | async-start | bytes 2162688 | tf_op jit(solution)/shard_map/all_gather | solution.py:32
  273.5 5.3 copy-start.2
  279.5 99.1 %all-gather.27.cloned.1.call-start = ((), (), s32[]{:S(2)}) async-start(), calls=%async_computation.6 | async-start | bytes 2162688 | tf_op jit(solution)/shard_map/all_gather | solution.py:32
  325.1 5.3 copy-start.16
  330.4 5.5 collective-permute-start.2
  336.7 93.6 %all-gather.29.cloned.1.call-start = ((), (), s32[]{:S(2)}) async-start(), calls=%async_computation.7 | async-start | bytes 2162688 | tf_op jit(solution)/shard_map/all_gather | solution.py:32
  381.0 5.3 copy-start
  387.0 161.4 %all-gather.31.cloned.1.call-start = ((), (), s32[]{:S(2)}) async-start(), calls=%async_computation.8 | async-start | bytes 2162688 | tf_op jit(solution)/shard_map/all_gather | solution.py:32
  432.6 5.3 copy-start.11
  432.6 70.6 %copy-start.17 = (f32[64]{0:T(128)S(1)}, f32[64]{0:T(128)}, u32[]{:S(2)}) copy-start(f32[64]{0:T(128)} %param.6) | copy-start | bytes 772
  503.3 5.5 collective-permute-start.3
  508.8 0.6 copy-start.6
  509.5 90.5 %all-gather.33.cloned.1.call-start = ((), (), s32[]{:S(2)}) async-start(), calls=%async_computation.9 | async-start | bytes 2162688 | tf_op jit(solution)/shard_map/all_gather | solution.py:32
  550.8 5.3 copy-start.7
  556.8 161.5 %all-gather.35.cloned.1.call-start = ((), (), s32[]{:S(2)}) async-start(), calls=%async_computation.10 | async-start | bytes 2162688 | tf_op jit(solution)/shard_map/all_gather | solution.py:32
  602.4 5.3 copy-start.13
  673.2 5.5 collective-permute-start.4
  678.7 0.6 copy-start.8
  679.4 90.5 %all-gather.37.cloned.1.call-start = ((), (), s32[]{:S(2)}) async-start(), calls=%async_computation.11 | async-start | bytes 2162688 | tf_op jit(solution)/shard_map/all_gather | solution.py:32
  720.7 5.3 copy-start.9
  726.7 161.5 %all-gather.39.cloned.1.call-start = ((), (), s32[]{:S(2)}) async-start(), calls=%async_computation.12 | async-start | bytes 2162688 | tf_op jit(solution)/shard_map/all_gather | solution.py:32
  772.3 5.3 copy-start.14
  843.1 5.5 collective-permute-start.5
  848.6 0.6 copy-start.4
  849.2 90.5 %all-gather.41.cloned.1.call-start = ((), (), s32[]{:S(2)}) async-start(), calls=%async_computation.13 | async-start | bytes 2162688 | tf_op jit(solution)/shard_map/all_gather | solution.py:32
  890.6 5.3 copy-start.5
  942.2 5.3 copy-start.12
  1013.0 5.5 collective-permute-start.6
  1018.5 5.5 collective-permute-start.7
Sparse Core Ops, SparseCore 0:
  9.7 46.2 all-gather.14
  64.5 43.0 all-gather.16
  121.7 41.8 all-gather.18
  172.1 43.0 all-gather.20
  229.2 41.8 all-gather.22
  279.6 43.0 all-gather.24
  336.8 41.8 all-gather.26
  387.2 43.0 all-gather.28
  509.6 38.7 all-gather.30
  557.0 43.0 all-gather.32
  679.5 38.7 all-gather.34
  726.8 43.0 all-gather.36
  849.4 38.7 all-gather.38
  896.7 43.0 all-gather.40
where the time goes:
time: 1030 us
  waiting for transfers between devices  623 us (60%)
  blocking collectives  261 us (25%)
  matrix products  74.5 us (7%)
  local copies, waits for them, and re-layouts  36.2 us (4%)
  between operations  13.7 us (1%)
  starting transfers between devices  12 us (1%)
  other arithmetic  10.6 us (1%)
    all_gather x14, waiting for transfers between devices, local(): whole = lax.all_gather(apply_state, 'grid', axis=1, tiled=True)  590 us
    psum x4, blocking collectives, local(): inventory = lax.psum(jnp.sum(held, axis=1), 'grid')  261 us
    dot_general x14, matrix products, local(): jnp.einsum('tbkc,bkrc->tbr', picked, blocks[apply_month_idx], precision=l...  74.5 us
    ppermute x8, waiting for transfers between devices, passed_along(): lax.ppermute(value, axis, [(i, (i + by) % devices) for i in range(devices)])  33 us
    reshape x14, local copies, waits for them, and re-layouts, local(): picked = whole.reshape(batch, -1, blk_size)[:, cols[apply_month_idx]]  24.5 us
  transfers between devices with their start and end apart: 22, of which 22 were waited for; matrix products, arithmetic and copies ran while one was open for 0% of the time, Pallas kernels for 0%

commit v1 on v0

v1 whole, which is shorter than its diff:
```python
import jax
import jax.numpy as jnp
from jax import lax
from jax.sharding import PartitionSpec as P

NBATCH = 2
PRECISION = lax.Precision.HIGHEST


def exchange(x, axis):
    return lax.all_to_all(x, axis, 0, 0, tiled=True)


def local(tracers, targets, retain, blocks, cols):
    sections = lax.axis_size("month")
    devices = lax.axis_size("grid")
    section = lax.axis_index("month")
    me = lax.axis_index("grid")
    months_here = blocks.shape[0]
    blk_count = blocks.shape[1]
    nk = blocks.shape[2]
    blk_size = blocks.shape[3]
    rows_here = blk_count * blk_size
    points = rows_here * devices
    tracer_count = tracers.shape[0]
    batch = tracer_count // NBATCH
    own = tracer_count // sections

    src_dev = cols // blk_count
    src_blk = cols % blk_count
    is_far = src_dev != me
    req = jnp.full((months_here, devices), -1, jnp.int32)
    for j in range(months_here):
        d = jnp.where(is_far[j], src_dev[j], devices).reshape(-1)
        req = req.at[j, d].set(src_blk[j].reshape(-1), mode="drop")
    want = exchange(req.T, "grid")
    send_idx = jnp.maximum(want, 0)
    pick = jnp.where(is_far, blk_count + src_dev, src_blk)

    def apply_month(state, j):
        sb = state.reshape(batch, blk_count, blk_size)
        out = jnp.take(sb, send_idx[:, j], axis=1)
        got = exchange(out.transpose(1, 0, 2), "grid").transpose(1, 0, 2)
        ext = jnp.concatenate([sb, got], axis=1)
        picked = jnp.take(ext, pick[j].reshape(-1), axis=1).reshape(batch, blk_count, nk, blk_size)
        mixed = jnp.einsum(
            "tbkc,bkrc->tbr",
            picked,
            blocks[j],
            precision=PRECISION,
            preferred_element_type=jnp.float32,
        )
        return retain[j][None, :] * state + mixed.reshape(batch, rows_here)

    held = jnp.zeros((batch, rows_here), jnp.float32)
    done = []
    steps = NBATCH + sections - 1
    for step in range(steps):
        if step < NBATCH:
            held = jnp.where(section == 0, tracers[step * batch : (step + 1) * batch], held)
        for j in range(months_here):
            held = apply_month(held, j)
        if step >= sections - 1:
            done.append(held)
        if step < steps - 1:
            held = lax.ppermute(held, "month", [(i, (i + 1) % sections) for i in range(sections)])
    final = jnp.concatenate(done, axis=0)
    part = jnp.sum(final, axis=1)
    inventory = jnp.sum(exchange(jnp.broadcast_to(part[None], (devices, tracer_count)), "grid"), axis=0)
    scaled = final * (targets * points / inventory)[:, None]
    result = scaled[(sections - 1) * own :]
    last = sections - 1
    for dst in range(sections - 1):
        moved = lax.ppermute(scaled[dst * own : (dst + 1) * own], "month", [(last, dst)])
        result = jnp.where(section == dst, moved, result)
    return result


def solution(mesh):
    return jax.shard_map(
        local,
        mesh=mesh,
        in_specs=(
            P(None, "grid"),
            P(),
            P("month", "grid"),
            P("month", "grid", None, None, None),
            P("month", "grid", None),
        ),
        out_specs=P("month", "grid"),
        check_vma=False,
    )
```

time: 1030 us -> 301 us (0.29)
  waiting for transfers between devices: 623 us -> 61.4 us
  blocking collectives: 261 us -> 129 us
  matrix products: 74.5 us -> 59.2 us
  local copies, waits for them, and re-layouts: 36.2 us -> 21.2 us
  between operations: 13.7 us -> 0.74 us
    all_gather x14 -> x0, waiting for transfers between devices: 590 us -> none  [local(): whole = lax.all_gather(apply_state, 'grid', axis=1, tiled=True)]
    psum x4 -> x0, blocking collectives: 261 us -> none  [local(): inventory = lax.psum(jnp.sum(held, axis=1), 'grid')]
    all_to_all x0 -> x9, blocking collectives: none -> 129 us  [exchange(): return lax.all_to_all(x, axis, 0, 0, tiled=True)]
    all_to_all x0 -> x3, waiting for transfers between devices: none -> 27.5 us  [exchange(): return lax.all_to_all(x, axis, 0, 0, tiled=True)]
    reshape x14 -> x4, local copies, waits for them, and re-layouts: 24.5 us -> 0.04 us  [apply_month(): sb = state.reshape(batch, blk_count, blk_size)]
    all_to_all x0 -> x3, starting transfers between devices: none -> 16.4 us  [exchange(): return lax.all_to_all(x, axis, 0, 0, tiled=True)]
    dot_general x14 -> x10, matrix products: 74.5 us -> 59.2 us  [apply_month(): jnp.einsum('tbkc,bkrc->tbr', picked, blocks[j], precision=PRECISION, pref...]
    ppermute x8 -> x7, waiting for transfers between devices: 33 us -> 33.9 us  [the longest x4 27.8 us: local(): lax.ppermute(held, 'month', [(i, (i + 1) % sections) for i in range(secti...]
  transfers between devices with their start and end apart: 22 -> 10, of which waited for: 22 -> 8; matrix products, arithmetic and copies ran while one was open for 0% -> 1% of each run, Pallas kernels for 0% -> 0%
where the time goes in v1:
time: 301 us; the launch traced here: 300 us
  blocking collectives  129 us (43%)
  waiting for transfers between devices  61.4 us (20%)
  matrix products  59.2 us (20%)
  local copies, waits for them, and re-layouts  21.2 us (7%)
  starting transfers between devices  21.1 us (7%)
  other arithmetic  7.41 us (2%)
    all_to_all x9, blocking collectives, exchange(): return lax.all_to_all(x, axis, 0, 0, tiled=True)  129 us
    dot_general x10, matrix products, apply_month(): jnp.einsum('tbkc,bkrc->tbr', picked, blocks[j], precision=PRECISION, pref...  59.2 us
    ppermute x4, waiting for transfers between devices, local(): lax.ppermute(held, 'month', [(i, (i + 1) % sections) for i in range(secti...  27.8 us
    all_to_all x3, waiting for transfers between devices, exchange(): return lax.all_to_all(x, axis, 0, 0, tiled=True)  27.5 us
    all_to_all x3, starting transfers between devices, exchange(): return lax.all_to_all(x, axis, 0, 0, tiled=True)  16.4 us
    scatter x2, local copies, waits for them, and re-layouts, local(): req = req.at[j, d].set(src_blk[j].reshape(-1), mode='drop')  6.94 us
    gather x10, local copies, waits for them, and re-layouts, apply_month(): jnp.take(ext, pick[j].reshape(-1), axis=1)  6.32 us
    ppermute x3, waiting for transfers between devices, local(): lax.ppermute(scaled[dst * own:(dst + 1) * own], 'month', [(last, dst)])  6.05 us
  transfers between devices with their start and end apart: 10, of which 8 were waited for; matrix products, arithmetic and copies ran while one was open for 1% of the time, Pallas kernels for 0%

profile of v1, /device:TPU:0, one launch (start us, length us, event | category | flops | bytes accessed | tf_op | source)
XLA Modules:
  0.0 300.3 jit_solution(9461408882457937265)
XLA Ops:
  0.0 0.8 add_select_fusion.2
  1.1 3.5 %scatter_fusion = s32[2,32]{1,0:T(2,128)S(1)} fusion(s32[2,32]{1,0:T(2,128)S(1)} %broadcast_in_dim.43, s32[64]{0:T(128)S(1)} %fusion.73, s32[64]{0:T(128)S(1)} %reshape.365), kind=kCustom, calls=%fused_computation.20 | custom fusion | bytes 1280 | tf_op jit(solution)/shard_map/scatter | solution.py:35
  4.6 3.5 %scatter_fusion.1 = s32[2,32]{1,0:T(2,128)S(1)} fusion(s32[2,32]{1,0:T(2,128)S(1)} %scatter_fusion, s32[64]{0:T(128)S(1)} %fusion.74, s32[64]{0:T(128)S(1)} %reshape.371), kind=kCustom, calls=%fused_computation.21 | custom fusion | bytes 1280 | tf_op jit(solution)/shard_map/scatter | solution.py:35
  8.1 0.7 copy.153
  8.8 8.4 %all-to-all-start = ((s32[32,1,2]{2,1,0:T(1,128)}), s32[32,1,2]{2,1,0:T(1,128)S(1)}, u32[]{:S(2)}, u32[]{:S(2)}) async-start(s32[32,1,2]{2,1,0:T(1,128)} %copy.153), calls=%async_computation | async-start | bytes 32768 | tf_op jit(solution)/shard_map/all_to_all | solution.py:11
  17.3 0.9 copy_bitcast_fusion.9
  18.3 6.2 %all-to-all-done = s32[32,1,2]{2,1,0:T(1,128)S(1)} async-done(((s32[32,1,2]{2,1,0:T(1,128)}), s32[32,1,2]{2,1,0:T(1,128)S(1)}, u32[]{:S(2)}, u32[]{:S(2)}) %all-to-all-start) | async-done | bytes 288 | tf_op jit(solution)/shard_map/all_to_all | solution.py:11
  24.7 0.6 gather_fusion
  25.3 0.9 broadcast_select_fusion.19
  26.2 3.9 %all-to-all-start.1 = ((f32[32,32,128]{2,1,0:T(8,128)}), f32[32,32,128]{2,1,0:T(8,128)S(1)}, u32[]{:S(2)}, u32[]{:S(2)}) async-start(f32[32,32,128]{2,1,0:T(8,128)} %broadcast_select_fusion.19), calls=%async_computation.1 | async-start | bytes 1048576 | tf_op jit(solution)/shard_map/all_to_all | solution.py:11
  30.1 0.8 fusion.76
  30.9 10.3 %all-to-all-done.1 = f32[32,32,128]{2,1,0:T(8,128)S(1)} async-done(((f32[32,32,128]{2,1,0:T(8,128)}), f32[32,32,128]{2,1,0:T(8,128)S(1)}, u32[]{:S(2)}, u32[]{:S(2)}) %all-to-all-start.1) | async-done | bytes 524320 | tf_op jit(solution)/shard_map/all_to_all | solution.py:11
  41.2 0.6 gather_fusion.1
  42.0 5.9 %fusion.30 = f32[8,4,8,128]{3,2,1,0:T(8,128)S(1)} fusion(f32[32,8,8,128]{3,0,2,1:T(8,128)S(1)} %bitcast.293, f32[2,8,8,128,128]{4,3,2,1,0:T(8,128)} %param.12), kind=kOutput, calls=%fused_computation.52 | convolution fusion | flops 402653184 | bytes 5373952 | tf_op jit(solution)/shard_map/tbkc,bkrc->tbr/dot_general | solution.py:46
  47.9 0.6 gather_fusion.2
  48.5 0.9 broadcast_select_fusion.18
  49.4 4.1 %all-to-all-start.2 = ((f32[32,32,128]{2,1,0:T(8,128)}), f32[32,32,128]{2,1,0:T(8,128)S(1)}, u32[]{:S(2)}, u32[]{:S(2)}) async-start(f32[32,32,128]{2,1,0:T(8,128)} %broadcast_select_fusion.18), calls=%async_computation.2 | async-start | bytes 1048576 | tf_op jit(solution)/shard_map/all_to_all | solution.py:11
  53.6 11.0 %all-to-all-done.2 = f32[32,32,128]{2,1,0:T(8,128)S(1)} async-done(((f32[32,32,128]{2,1,0:T(8,128)}), f32[32,32,128]{2,1,0:T(8,128)S(1)}, u32[]{:S(2)}, u32[]{:S(2)}) %all-to-all-start.2) | async-done | bytes 524320 | tf_op jit(solution)/shard_map/all_to_all | solution.py:11
  64.7 0.6 gather_fusion.3
  65.4 5.9 %fusion.45 = f32[8,4,8,128]{3,2,1,0:T(8,128)S(1)} fusion(f32[32,8,8,128]{3,0,2,1:T(8,128)S(1)} %bitcast.294, f32[2,8,8,128,128]{4,3,2,1,0:T(8,128)} %param.12), kind=kOutput, calls=%fused_computation.57 | convolution fusion | flops 402653184 | bytes 5373952 | tf_op jit(solution)/shard_map/tbkc,bkrc->tbr/dot_general | solution.py:46
  71.4 1.6 collective-permute-start
  73.0 5.9 %collective-permute-done = f32[32,1024]{1,0:T(8,128)S(1)} collective-permute-done((f32[32,1024]{1,0:T(8,128)S(1)}, f32[32,1024]{1,0:T(8,128)S(1)}, u32[]{:S(2)}, u32[]{:S(2)}) %collective-permute-start) | collective-permute-done | bytes 131104 | tf_op jit(solution)/shard_map/ppermute | solution.py:66
  78.9 0.6 gather_fusion.4
  79.6 14.5 %all_to_all.65 = f32[32,32,128]{2,1,0:T(8,128)S(1)} all-to-all(f32[32,32,128]{2,1,0:T(8,128)S(1)} %broadcast_select_fusion.17), channel_id=1, replica_groups=mesh['month'=4,'grid'=32] {'grid'}, dimensions={0} | all-to-all | bytes 1048576 | tf_op jit(solution)/shard_map/all_to_all | solution.py:11
  94.1 0.6 gather_fusion.5
  94.9 5.9 %fusion.33 = f32[8,4,8,128]{3,2,1,0:T(8,128)S(1)} fusion(f32[32,8,8,128]{3,0,2,1:T(8,128)S(1)} %bitcast.295, f32[2,8,8,128,128]{4,3,2,1,0:T(8,128)} %param.12), kind=kOutput, calls=%fused_computation.53 | convolution fusion | flops 402653184 | bytes 5373952 | tf_op jit(solution)/shard_map/tbkc,bkrc->tbr/dot_general | solution.py:46
  100.9 0.6 gather_fusion.6
  101.6 15.0 %all_to_all.66 = f32[32,32,128]{2,1,0:T(8,128)S(1)} all-to-all(f32[32,32,128]{2,1,0:T(8,128)S(1)} %broadcast_select_fusion.16), channel_id=1, replica_groups=mesh['month'=4,'grid'=32] {'grid'}, dimensions={0} | all-to-all | bytes 1048576 | tf_op jit(solution)/shard_map/all_to_all | solution.py:11
  116.7 0.6 gather_fusion.7
  117.5 5.9 %fusion.48 = f32[8,4,8,128]{3,2,1,0:T(8,128)S(1)} fusion(f32[32,8,8,128]{3,0,2,1:T(8,128)S(1)} %bitcast.296, f32[2,8,8,128,128]{4,3,2,1,0:T(8,128)} %param.12), kind=kOutput, calls=%fused_computation.58 | convolution fusion | flops 402653184 | bytes 5373952 | tf_op jit(solution)/shard_map/tbkc,bkrc->tbr/dot_general | solution.py:46
  123.4 0.3 collective-permute-start.1
  123.8 7.1 %collective-permute-done.1 = f32[32,1024]{1,0:T(8,128)S(1)} collective-permute-done((f32[32,1024]{1,0:T(8,128)S(1)}, f32[32,1024]{1,0:T(8,128)S(1)}, u32[]{:S(2)}, u32[]{:S(2)}) %collective-permute-start.1) | collective-permute-done | bytes 131104 | tf_op jit(solution)/shard_map/ppermute | solution.py:66
  130.9 0.6 gather_fusion.8
  131.6 14.5 %all_to_all.67 = f32[32,32,128]{2,1,0:T(8,128)S(1)} all-to-all(f32[32,32,128]{2,1,0:T(8,128)S(1)} %broadcast_select_fusion.15), channel_id=1, replica_groups=mesh['month'=4,'grid'=32] {'grid'}, dimensions={0} | all-to-all | bytes 1048576 | tf_op jit(solution)/shard_map/all_to_all | solution.py:11
  146.1 0.6 gather_fusion.9
  146.9 5.9 %fusion.36 = f32[8,4,8,128]{3,2,1,0:T(8,128)S(1)} fusion(f32[32,8,8,128]{3,0,2,1:T(8,128)S(1)} %bitcast.297, f32[2,8,8,128,128]{4,3,2,1,0:T(8,128)} %param.12), kind=kOutput, calls=%fused_computation.54 | convolution fusion | flops 402653184 | bytes 5373952 | tf_op jit(solution)/shard_map/tbkc,bkrc->tbr/dot_general | solution.py:46
  152.9 0.6 gather_fusion.10
  153.6 15.0 %all_to_all.68 = f32[32,32,128]{2,1,0:T(8,128)S(1)} all-to-all(f32[32,32,128]{2,1,0:T(8,128)S(1)} %broadcast_select_fusion.14), channel_id=1, replica_groups=mesh['month'=4,'grid'=32] {'grid'}, dimensions={0} | all-to-all | bytes 1048576 | tf_op jit(solution)/shard_map/all_to_all | solution.py:11
  168.6 0.6 gather_fusion.11
  169.4 5.9 %fusion.51 = f32[8,4,8,128]{3,2,1,0:T(8,128)S(1)} fusion(f32[32,8,8,128]{3,0,2,1:T(8,128)S(1)} %bitcast.298, f32[2,8,8,128,128]{4,3,2,1,0:T(8,128)} %param.12), kind=kOutput, calls=%fused_computation.59 | convolution fusion | flops 402653184 | bytes 5373952 | tf_op jit(solution)/shard_map/tbkc,bkrc->tbr/dot_general | solution.py:46
  175.5 7.4 %collective-permute-done.2 = f32[32,1024]{1,0:T(8,128)S(1)} collective-permute-done((f32[32,1024]{1,0:T(8,128)S(1)}, f32[32,1024]{1,0:T(8,128)S(1)}, u32[]{:S(2)}, u32[]{:S(2)}) %collective-permute-start.2) | collective-permute-done | bytes 131104 | tf_op jit(solution)/shard_map/ppermute | solution.py:66
  182.9 0.6 gather_fusion.12
  183.6 14.5 %all_to_all.69 = f32[32,32,128]{2,1,0:T(8,128)S(1)} all-to-all(f32[32,32,128]{2,1,0:T(8,128)S(1)} %broadcast_select_fusion.13), channel_id=1, replica_groups=mesh['month'=4,'grid'=32] {'grid'}, dimensions={0} | all-to-all | bytes 1048576 | tf_op jit(solution)/shard_map/all_to_all | solution.py:11
  198.1 0.6 gather_fusion.13
  198.9 5.9 %fusion.39 = f32[8,4,8,128]{3,2,1,0:T(8,128)S(1)} fusion(f32[32,8,8,128]{3,0,2,1:T(8,128)S(1)} %bitcast.299, f32[2,8,8,128,128]{4,3,2,1,0:T(8,128)} %param.12), kind=kOutput, calls=%fused_computation.55 | convolution fusion | flops 402653184 | bytes 5373952 | tf_op jit(solution)/shard_map/tbkc,bkrc->tbr/dot_general | solution.py:46
  204.8 0.6 gather_fusion.14
  205.5 15.0 %all_to_all.70 = f32[32,32,128]{2,1,0:T(8,128)S(1)} all-to-all(f32[32,32,128]{2,1,0:T(8,128)S(1)} %broadcast_select_fusion.12), channel_id=1, replica_groups=mesh['month'=4,'grid'=32] {'grid'}, dimensions={0} | all-to-all | bytes 1048576 | tf_op jit(solution)/shard_map/all_to_all | solution.py:11
  220.6 0.6 gather_fusion.15
  221.4 5.9 %fusion.54 = f32[8,4,8,128]{3,2,1,0:T(8,128)S(1)} fusion(f32[32,8,8,128]{3,0,2,1:T(8,128)S(1)} %bitcast.300, f32[2,8,8,128,128]{4,3,2,1,0:T(8,128)} %param.12), kind=kOutput, calls=%fused_computation.60 | convolution fusion | flops 402653184 | bytes 5373952 | tf_op jit(solution)/shard_map/tbkc,bkrc->tbr/dot_general | solution.py:46
  227.4 7.4 %collective-permute-done.3 = f32[32,1024]{1,0:T(8,128)S(1)} collective-permute-done((f32[32,1024]{1,0:T(8,128)S(1)}, f32[32,1024]{1,0:T(8,128)S(1)}, u32[]{:S(2)}, u32[]{:S(2)}) %collective-permute-start.3) | collective-permute-done | bytes 131104 | tf_op jit(solution)/shard_map/ppermute | solution.py:66
  234.9 0.6 gather_fusion.16
  235.6 14.5 %all_to_all.71 = f32[32,32,128]{2,1,0:T(8,128)S(1)} all-to-all(f32[32,32,128]{2,1,0:T(8,128)S(1)} %broadcast_select_fusion.11), channel_id=1, replica_groups=mesh['month'=4,'grid'=32] {'grid'}, dimensions={0} | all-to-all | bytes 1048576 | tf_op jit(solution)/shard_map/all_to_all | solution.py:11
  250.1 0.6 gather_fusion.17
  250.9 5.9 %fusion.42 = f32[8,4,8,128]{3,2,1,0:T(8,128)S(1)} fusion(f32[32,8,8,128]{3,0,2,1:T(8,128)S(1)} %bitcast.291, f32[2,8,8,128,128]{4,3,2,1,0:T(8,128)} %param.12), kind=kOutput, calls=%fused_computation.56 | convolution fusion | flops 402653184 | bytes 5373952 | tf_op jit(solution)/shard_map/tbkc,bkrc->tbr/dot_general | solution.py:46
  256.8 0.6 gather_fusion.18
  257.5 15.0 %all_to_all.72 = f32[32,32,128]{2,1,0:T(8,128)S(1)} all-to-all(f32[32,32,128]{2,1,0:T(8,128)S(1)} %broadcast_select_fusion.10), channel_id=1, replica_groups=mesh['month'=4,'grid'=32] {'grid'}, dimensions={0} | all-to-all | bytes 1048576 | tf_op jit(solution)/shard_map/all_to_all | solution.py:11
  272.6 0.6 gather_fusion.19
  273.4 5.9 %fusion.57 = f32[8,4,8,128]{3,2,1,0:T(8,128)S(1)} fusion(f32[32,8,8,128]{3,0,2,1:T(8,128)S(1)} %bitcast.292, f32[2,8,8,128,128]{4,3,2,1,0:T(8,128)} %param.12), kind=kOutput, calls=%fused_computation.61 | convolution fusion | flops 402653184 | bytes 5373952 | tf_op jit(solution)/shard_map/tbkc,bkrc->tbr/dot_general | solution.py:46
  279.5 11.3 %all_to_all.73 = f32[32,1,64]{2,1,0:T(1,128)S(1)} all-to-all(f32[32,1,64]{2,1,0:T(1,128)S(1)} %broadcast_in_dim.46), channel_id=1, replica_groups=mesh['month'=4,'grid'=32] {'grid'}, dimensions={0} | all-to-all | bytes 16384 | tf_op jit(solution)/shard_map/all_to_all | solution.py:11
  291.0 0.7 collective-permute-start.4
  291.6 0.7 collective-permute-start.5
  292.3 1.3 collective-permute-start.6
  293.6 6.0 %collective-permute-done.6 = f32[16,1024]{1,0:T(8,128)S(1)} collective-permute-done((f32[16,1024]{1,0:T(8,128)S(1)}, f32[16,1024]{1,0:T(8,128)S(1)}, u32[]{:S(2)}, u32[]{:S(2)}) %collective-permute-start.6) | collective-permute-done | bytes 65568 | tf_op jit(solution)/shard_map/ppermute | solution.py:74
  299.7 0.6 fusion.64
  (80 shorter events, 4.1 us)
Async XLA Ops:
  0.0 47.9 %copy-start = (f32[64,1024]{1,0:T(8,128)S(1)}, f32[64,1024]{1,0:T(8,128)}, u32[]{:S(2)}) copy-start(f32[64,1024]{1,0:T(8,128)} %param.9) | copy-start | bytes 786436
  8.8 15.8 %all-to-all-start = ((s32[32,1,2]{2,1,0:T(1,128)}), s32[32,1,2]{2,1,0:T(1,128)S(1)}, u32[]{:S(2)}, u32[]{:S(2)}) async-start(s32[32,1,2]{2,1,0:T(1,128)} %copy.153), calls=%async_computation | async-start | bytes 32768 | tf_op jit(solution)/shard_map/all_to_all | solution.py:11
  26.2 15.0 %all-to-all-start.1 = ((f32[32,32,128]{2,1,0:T(8,128)}), f32[32,32,128]{2,1,0:T(8,128)S(1)}, u32[]{:S(2)}, u32[]{:S(2)}) async-start(f32[32,32,128]{2,1,0:T(8,128)} %broadcast_select_fusion.19), calls=%async_computation.1 | async-start | bytes 1048576 | tf_op jit(solution)/shard_map/all_to_all | solution.py:11
  49.4 15.2 %all-to-all-start.2 = ((f32[32,32,128]{2,1,0:T(8,128)}), f32[32,32,128]{2,1,0:T(8,128)S(1)}, u32[]{:S(2)}, u32[]{:S(2)}) async-start(f32[32,32,128]{2,1,0:T(8,128)} %broadcast_select_fusion.18), calls=%async_computation.2 | async-start | bytes 1048576 | tf_op jit(solution)/shard_map/all_to_all | solution.py:11
  71.4 7.5 %collective-permute-start = (f32[32,1024]{1,0:T(8,128)S(1)}, f32[32,1024]{1,0:T(8,128)S(1)}, u32[]{:S(2)}, u32[]{:S(2)}) collective-permute-start(f32[32,1024]{1,0:T(8,128)S(1)} %bitcast_add_fusion.8), channel_id=1, source_target_pairs={{0,32},{32,64},{64,96},{96,0},{1,33},{33,65},{65,97},{97,1},{2,34}... | collective-permute-start | bytes 393224 | tf_op jit(solution)/shard_map/ppermute | solution.py:66
  123.4 7.5 %collective-permute-start.1 = (f32[32,1024]{1,0:T(8,128)S(1)}, f32[32,1024]{1,0:T(8,128)S(1)}, u32[]{:S(2)}, u32[]{:S(2)}) collective-permute-start(f32[32,1024]{1,0:T(8,128)S(1)} %bitcast_add_fusion.6), channel_id=1, source_target_pairs={{0,32},{32,64},{64,96},{96,0},{1,33},{33,65},{65,97},{97,1},{2,34}... | collective-permute-start | bytes 393224 | tf_op jit(solution)/shard_map/ppermute | solution.py:66
  175.4 7.5 %collective-permute-start.2 = (f32[32,1024]{1,0:T(8,128)S(1)}, f32[32,1024]{1,0:T(8,128)S(1)}, u32[]{:S(2)}, u32[]{:S(2)}) collective-permute-start(f32[32,1024]{1,0:T(8,128)S(1)} %bitcast_add_fusion.4), channel_id=1, source_target_pairs={{0,32},{32,64},{64,96},{96,0},{1,33},{33,65},{65,97},{97,1},{2,34}... | collective-permute-start | bytes 393224 | tf_op jit(solution)/shard_map/ppermute | solution.py:66
  227.4 7.5 %collective-permute-start.3 = (f32[32,1024]{1,0:T(8,128)S(1)}, f32[32,1024]{1,0:T(8,128)S(1)}, u32[]{:S(2)}, u32[]{:S(2)}) collective-permute-start(f32[32,1024]{1,0:T(8,128)S(1)} %bitcast_add_fusion.2), channel_id=1, source_target_pairs={{0,32},{32,64},{64,96},{96,0},{1,33},{33,65},{65,97},{97,1},{2,34}... | collective-permute-start | bytes 393224 | tf_op jit(solution)/shard_map/ppermute | solution.py:66
  256.8 34.1 %copy-start.1 = (f32[64]{0:T(128)S(1)}, f32[64]{0:T(128)}, u32[]{:S(2)}) copy-start(f32[64]{0:T(128)} %param.10) | copy-start | bytes 772
  291.0 2.7 collective-permute-start.4
  291.6 2.0 collective-permute-start.5
  292.3 7.4 %collective-permute-start.6 = (f32[16,1024]{1,0:T(8,128)S(1)}, f32[16,1024]{1,0:T(8,128)S(1)}, u32[]{:S(2)}, u32[]{:S(2)}) collective-permute-start(f32[16,1024]{1,0:T(8,128)S(1)} %get-tuple-element.13), channel_id=1, source_target_pairs={{96,0},{97,1},{98,2},{99,3},{100,4},{101,5},{102,6},{103,7},{104,8... | collective-permute-start | bytes 196616 | tf_op jit(solution)/shard_map/ppermute | solution.py:74

commit v2 on v1

v2 whole, which is shorter than its diff:
```python
import jax
import jax.numpy as jnp
from jax import lax
from jax.sharding import PartitionSpec as P

NBATCH = 2
PRECISION = lax.Precision.HIGH
FAR = 2


def exchange(x, axis):
    return lax.all_to_all(x, axis, 0, 0, tiled=True)


def local(tracers, targets, retain, blocks, cols):
    sections = lax.axis_size("month")
    devices = lax.axis_size("grid")
    section = lax.axis_index("month")
    me = lax.axis_index("grid")
    months_here = blocks.shape[0]
    blk_count = blocks.shape[1]
    nk = blocks.shape[2]
    blk_size = blocks.shape[3]
    rows_here = blk_count * blk_size
    points = rows_here * devices
    tracer_count = tracers.shape[0]
    batch = tracer_count // NBATCH
    own = tracer_count // sections

    src_dev = cols // blk_count
    src_blk = cols % blk_count
    near = nk - FAR
    far_dev = src_dev[:, :, near:].reshape(months_here, -1)
    far_blk = src_blk[:, :, near:].reshape(months_here, -1)
    hit = far_dev[:, None, :] == jnp.arange(devices, dtype=jnp.int32)[None, :, None]
    req = jnp.sum(jnp.where(hit, far_blk[:, None, :] + 1, 0), axis=2) - 1

    last_m = months_here - 1
    colsum = jnp.sum(blocks[last_m], axis=2)
    to_blk = src_blk[last_m, :, :near][:, :, None] == jnp.arange(blk_count, dtype=jnp.int32)[None, None, :]
    c_loc = jnp.sum(jnp.where(to_blk[:, :, :, None], colsum[:, :near, None, :], 0.0), axis=(0, 1))
    far_cs = colsum[:, near:].reshape(-1, blk_size)
    cs_send = jnp.sum(jnp.where(hit[last_m][:, :, None], far_cs[None], 0.0), axis=1)
    sent = jnp.concatenate([cs_send, req.T.astype(jnp.float32)], axis=1)
    recv = exchange(sent, "grid")
    want = jnp.round(recv[:, blk_size:]).astype(jnp.int32)
    send_idx = jnp.maximum(want, 0)
    from_e = want[:, last_m][:, None] == jnp.arange(blk_count, dtype=jnp.int32)[None, :]
    c_far = jnp.sum(jnp.where(from_e[:, :, None], recv[:, None, :blk_size], 0.0), axis=0)
    c_all = (retain[last_m].reshape(blk_count, blk_size) + c_loc + c_far).reshape(rows_here)

    def apply_month(state, j):
        sb = state.reshape(batch, blk_count, blk_size)
        out = jnp.take(sb, send_idx[:, j], axis=1).transpose(1, 0, 2)
        if j == last_m:
            part = jnp.sum(state * c_all[None, :], axis=1)
            row = jnp.zeros((devices, 8, blk_size), jnp.float32).at[:, 0, :batch].set(part[None, :])
            full = exchange(jnp.concatenate([out, row], axis=1), "grid")
            inventory = jnp.sum(full[:, batch, :batch], axis=0)
            got = full[:, :batch].transpose(1, 0, 2)
        else:
            inventory = None
            got = exchange(out, "grid").transpose(1, 0, 2)
        loc = jnp.take(sb, src_blk[j, :, :near].reshape(-1), axis=1).reshape(batch, blk_count, near, blk_size)
        far = jnp.take(got, src_dev[j, :, near:].reshape(-1), axis=1).reshape(batch, blk_count, FAR, blk_size)
        mixed = jnp.einsum(
            "tbkc,bkrc->tbr",
            loc,
            blocks[j, :, :near],
            precision=PRECISION,
            preferred_element_type=jnp.float32,
        ) + jnp.einsum(
            "tbkc,bkrc->tbr",
            far,
            blocks[j, :, near:],
            precision=PRECISION,
            preferred_element_type=jnp.float32,
        )
        return retain[j][None, :] * state + mixed.reshape(batch, rows_here), inventory

    held = jnp.zeros((batch, rows_here), jnp.float32)
    result = jnp.zeros((own, rows_here), jnp.float32)
    last = sections - 1
    steps = NBATCH + sections - 1
    for step in range(steps):
        if step < NBATCH:
            held = jnp.where(section == 0, tracers[step * batch : (step + 1) * batch], held)
        for j in range(months_here):
            held, inventory = apply_month(held, j)
        b = step - last
        if b >= 0:
            scaled = held * (targets[b * batch : (b + 1) * batch] * points / inventory)[:, None]
            for q in range(batch // own):
                owner = (b * batch + q * own) // own
                piece = scaled[q * own : (q + 1) * own]
                if owner != last:
                    piece = lax.ppermute(piece, "month", [(last, owner)])
                result = jnp.where(section == owner, piece, result)
        if step < steps - 1:
            held = lax.ppermute(held, "month", [(i, (i + 1) % sections) for i in range(sections)])
    return result


def solution(mesh):
    return jax.shard_map(
        local,
        mesh=mesh,
        in_specs=(
            P(None, "grid"),
            P(),
            P("month", "grid"),
            P("month", "grid", None, None, None),
            P("month", "grid", None),
        ),
        out_specs=P("month", "grid"),
        check_vma=False,
    )
```

time: 301 us -> 261 us (0.87); the launches traced: 300 us -> 257 us
  blocking collectives: 129 us -> 0 us
  waiting for transfers between devices: 61.4 us -> 108 us
  starting transfers between devices: 21.1 us -> 55.6 us
  other arithmetic: 7.41 us -> 18.5 us
  matrix products: 59.2 us -> 53.9 us
    all_to_all x9 -> x0, blocking collectives: 129 us -> none  [exchange(): return lax.all_to_all(x, axis, 0, 0, tiled=True)]
    all_to_all x3 -> x11, waiting for transfers between devices: 27.5 us -> 80.8 us  [exchange(): return lax.all_to_all(x, axis, 0, 0, tiled=True)]
    all_to_all x3 -> x11, starting transfers between devices: 16.4 us -> 50.9 us  [exchange(): return lax.all_to_all(x, axis, 0, 0, tiled=True)]
    scatter x2 -> x10, local copies, waits for them, and re-layouts: 6.94 us -> 0.09 us  [apply_month(): jnp.zeros((devices, 8, blk_size), jnp.float32).at[:, 0, :batch]]
    ppermute x3, waiting for transfers between devices: 6.05 us -> 0.01 us  [local(): piece = lax.ppermute(piece, 'month', [(last, owner)])]
    gather x20 -> x30, local copies, waits for them, and re-layouts: 12.2 us -> 17.6 us  [the longest x10 6.09 us: apply_month(): jnp.take(sb, src_blk[j, :, :near].reshape(-1), axis=1)]
    dot_general x10 -> x20, matrix products: 59.2 us -> 53.9 us  [the longest x10 35.3 us: apply_month(): jnp.einsum('tbkc,bkrc->tbr', loc, blocks[j, :, :near], precision=PRECISIO...]
    concatenate x12 -> x6, other arithmetic: 0.47 us -> 4.43 us  [the longest x5 4.42 us: apply_month(): full = exchange(jnp.concatenate([out, row], axis=1), 'grid')]
  transfers between devices with their start and end apart: 10 -> 18, of which waited for: 8 -> 15; matrix products, arithmetic and copies ran while one was open for 1% -> 17% of each run, Pallas kernels for 0% -> 0%
where the time goes in v2:
time: 261 us; the launch traced here: 257 us
  waiting for transfers between devices  108 us (41%)
  starting transfers between devices  55.6 us (21%)
  matrix products  53.9 us (21%)
  local copies, waits for them, and re-layouts  19.9 us (8%)
  other arithmetic  18.5 us (7%)
    all_to_all x11, waiting for transfers between devices, exchange(): return lax.all_to_all(x, axis, 0, 0, tiled=True)  80.8 us
    all_to_all x11, starting transfers between devices, exchange(): return lax.all_to_all(x, axis, 0, 0, tiled=True)  50.9 us
    dot_general x10, matrix products, apply_month(): jnp.einsum('tbkc,bkrc->tbr', loc, blocks[j, :, :near], precision=PRECISIO...  35.3 us
    ppermute x4, waiting for transfers between devices, local(): lax.ppermute(held, 'month', [(i, (i + 1) % sections) for i in range(secti...  27.3 us
    dot_general x10, matrix products, apply_month(): jnp.einsum('tbkc,bkrc->tbr', far, blocks[j, :, near:], precision=PRECISIO...  18.6 us
    gather x10, local copies, waits for them, and re-layouts, apply_month(): jnp.take(sb, src_blk[j, :, :near].reshape(-1), axis=1)  6.09 us
    gather x10, local copies, waits for them, and re-layouts, apply_month(): out = jnp.take(sb, send_idx[:, j], axis=1).transpose(1, 0, 2)  5.88 us
    gather x10, local copies, waits for them, and re-layouts, apply_month(): jnp.take(got, src_dev[j, :, near:].reshape(-1), axis=1)  5.67 us
  transfers between devices with their start and end apart: 18, of which 15 were waited for; matrix products, arithmetic and copies ran while one was open for 17% of the time, Pallas kernels for 0%

profile of v2, /device:TPU:0, one launch (start us, length us, event | category | flops | bytes accessed | tf_op | source)
XLA Modules:
  0.0 257.1 jit_solution(9300801472665738605)
XLA Ops:
  0.0 0.7 add_select_fusion
  1.4 2.7 %slice_reduce_fusion = f32[8,8,128]{2,1,0:T(8,128)S(1)} fusion(f32[2,8,8,128,128]{4,3,2,1,0:T(8,128)} %param.24), kind=kLoop, calls=%fused_computation.30 | loop fusion | flops 1040384 | bytes 4227072 | tf_op jit(solution)/shard_map/reduce_sum | solution.py:39
  4.9 8.4 %all-to-all-start = ((f32[32,1,130]{2,1,0:T(1,128)}), f32[32,1,130]{2,1,0:T(1,128)S(1)}, u32[]{:S(2)}, u32[]{:S(2)}) async-start(f32[32,1,130]{2,1,0:T(1,128)} %all_to_all.38), calls=%async_computation | async-start | bytes 65536 | tf_op jit(solution)/shard_map/all_to_all | solution.py:12
  14.0 0.9 copy_bitcast_fusion.9
  15.7 3.5 %fusion.50 = f32[8,32,128]{2,1,0:T(8,128)S(1)} fusion(f32[32,8,6,128]{3,0,2,1:T(8,128)S(1)} %bitcast.420, f32[2,8,8,128,128]{4,3,2,1,0:T(8,128)} %param.24), kind=kOutput, calls=%fused_computation.91 | convolution fusion | flops 150994944 | bytes 4063232 | tf_op jit(solution)/shard_map/tbkc,bkrc->tbr/dot_general | solution.py:66
  19.3 1.5 all-to-all-done
  21.9 0.9 broadcast_select_fusion.19
  22.8 5.9 %all-to-all-start.1 = ((f32[32,32,128]{2,1,0:T(8,128)}), f32[32,32,128]{2,1,0:T(8,128)S(1)}, u32[]{:S(2)}, u32[]{:S(2)}) async-start(f32[32,32,128]{2,1,0:T(8,128)} %broadcast_select_fusion.19), calls=%async_computation.1 | async-start | bytes 1048576 | tf_op jit(solution)/shard_map/all_to_all | solution.py:12
  28.9 10.9 %all-to-all-done.1 = f32[32,32,128]{2,1,0:T(8,128)S(1)} async-done(((f32[32,32,128]{2,1,0:T(8,128)}), f32[32,32,128]{2,1,0:T(8,128)S(1)}, u32[]{:S(2)}, u32[]{:S(2)}) %all-to-all-start.1) | async-done | bytes 524320 | tf_op jit(solution)/shard_map/all_to_all | solution.py:12
  40.5 1.9 fusion.40
  43.3 0.9 pad_maximum_fusion
  44.2 4.1 %all-to-all-start.2 = ((f32[32,40,128]{2,1,0:T(8,128)}), f32[32,40,128]{2,1,0:T(8,128)S(1)}, u32[]{:S(2)}, u32[]{:S(2)}) async-start(f32[32,40,128]{2,1,0:T(8,128)} %pad_maximum_fusion), calls=%async_computation.2 | async-start | bytes 1310720 | tf_op jit(solution)/shard_map/all_to_all | solution.py:12
  49.1 3.5 %fusion.65 = f32[8,32,128]{2,1,0:T(8,128)S(1)} fusion(f32[32,8,6,128]{3,0,2,1:T(8,128)S(1)} %bitcast.421, f32[2,8,8,128,128]{4,3,2,1,0:T(8,128)} %param.24), kind=kOutput, calls=%fused_computation.96 | convolution fusion | flops 150994944 | bytes 4063232 | tf_op jit(solution)/shard_map/tbkc,bkrc->tbr/dot_general | solution.py:66
  52.6 8.2 %all-to-all-done.2 = f32[32,40,128]{2,1,0:T(8,128)S(1)} async-done(((f32[32,40,128]{2,1,0:T(8,128)}), f32[32,40,128]{2,1,0:T(8,128)S(1)}, u32[]{:S(2)}, u32[]{:S(2)}) %all-to-all-start.2) | async-done | bytes 655392 | tf_op jit(solution)/shard_map/all_to_all | solution.py:12
  61.6 1.9 fusion.41
  63.5 1.6 collective-permute-start
  65.0 5.8 %collective-permute-done = f32[32,1024]{1,0:T(8,128)S(1)} collective-permute-done((f32[32,1024]{1,0:T(8,128)S(1)}, f32[32,1024]{1,0:T(8,128)S(1)}, u32[]{:S(2)}, u32[]{:S(2)}) %collective-permute-start) | collective-permute-done | bytes 131104 | tf_op jit(solution)/shard_map/ppermute | solution.py:100
  72.0 0.9 broadcast_select_fusion.17
  72.9 3.9 %all-to-all-start.3 = ((f32[32,32,128]{2,1,0:T(8,128)}), f32[32,32,128]{2,1,0:T(8,128)S(1)}, u32[]{:S(2)}, u32[]{:S(2)}) async-start(f32[32,32,128]{2,1,0:T(8,128)} %broadcast_select_fusion.17), calls=%async_computation.3 | async-start | bytes 1048576 | tf_op jit(solution)/shard_map/all_to_all | solution.py:12
  76.9 3.5 %fusion.53 = f32[8,32,128]{2,1,0:T(8,128)S(1)} fusion(f32[32,8,6,128]{3,0,2,1:T(8,128)S(1)} %bitcast.422, f32[2,8,8,128,128]{4,3,2,1,0:T(8,128)} %param.24), kind=kOutput, calls=%fused_computation.92 | convolution fusion | flops 150994944 | bytes 4063232 | tf_op jit(solution)/shard_map/tbkc,bkrc->tbr/dot_general | solution.py:66
  80.5 7.4 %all-to-all-done.3 = f32[32,32,128]{2,1,0:T(8,128)S(1)} async-done(((f32[32,32,128]{2,1,0:T(8,128)}), f32[32,32,128]{2,1,0:T(8,128)S(1)}, u32[]{:S(2)}, u32[]{:S(2)}) %all-to-all-start.3) | async-done | bytes 524320 | tf_op jit(solution)/shard_map/all_to_all | solution.py:12
  88.5 1.9 fusion.42
  91.3 0.9 pad_maximum_fusion.1
  92.2 4.3 %all-to-all-start.4 = ((f32[32,40,128]{2,1,0:T(8,128)}), f32[32,40,128]{2,1,0:T(8,128)S(1)}, u32[]{:S(2)}, u32[]{:S(2)}) async-start(f32[32,40,128]{2,1,0:T(8,128)} %pad_maximum_fusion.1), calls=%async_computation.4 | async-start | bytes 1310720 | tf_op jit(solution)/shard_map/all_to_all | solution.py:12
  97.2 3.5 %fusion.68 = f32[8,32,128]{2,1,0:T(8,128)S(1)} fusion(f32[32,8,6,128]{3,0,2,1:T(8,128)S(1)} %bitcast.423, f32[2,8,8,128,128]{4,3,2,1,0:T(8,128)} %param.24), kind=kOutput, calls=%fused_computation.97 | convolution fusion | flops 150994944 | bytes 4063232 | tf_op jit(solution)/shard_map/tbkc,bkrc->tbr/dot_general | solution.py:66
  100.8 8.1 %all-to-all-done.4 = f32[32,40,128]{2,1,0:T(8,128)S(1)} async-done(((f32[32,40,128]{2,1,0:T(8,128)}), f32[32,40,128]{2,1,0:T(8,128)S(1)}, u32[]{:S(2)}, u32[]{:S(2)}) %all-to-all-start.4) | async-done | bytes 655392 | tf_op jit(solution)/shard_map/all_to_all | solution.py:12
  109.6 1.9 fusion.43
  111.8 7.0 %collective-permute-done.1 = f32[32,1024]{1,0:T(8,128)S(1)} collective-permute-done((f32[32,1024]{1,0:T(8,128)S(1)}, f32[32,1024]{1,0:T(8,128)S(1)}, u32[]{:S(2)}, u32[]{:S(2)}) %collective-permute-start.1) | collective-permute-done | bytes 131104 | tf_op jit(solution)/shard_map/ppermute | solution.py:100
  120.0 0.9 broadcast_select_fusion.15
  120.9 3.9 %all-to-all-start.5 = ((f32[32,32,128]{2,1,0:T(8,128)}), f32[32,32,128]{2,1,0:T(8,128)S(1)}, u32[]{:S(2)}, u32[]{:S(2)}) async-start(f32[32,32,128]{2,1,0:T(8,128)} %broadcast_select_fusion.15), calls=%async_computation.5 | async-start | bytes 1048576 | tf_op jit(solution)/shard_map/all_to_all | solution.py:12
  124.9 3.5 %fusion.56 = f32[8,32,128]{2,1,0:T(8,128)S(1)} fusion(f32[32,8,6,128]{3,0,2,1:T(8,128)S(1)} %bitcast.424, f32[2,8,8,128,128]{4,3,2,1,0:T(8,128)} %param.24), kind=kOutput, calls=%fused_computation.93 | convolution fusion | flops 150994944 | bytes 4063232 | tf_op jit(solution)/shard_map/tbkc,bkrc->tbr/dot_general | solution.py:66
  128.5 7.4 %all-to-all-done.5 = f32[32,32,128]{2,1,0:T(8,128)S(1)} async-done(((f32[32,32,128]{2,1,0:T(8,128)}), f32[32,32,128]{2,1,0:T(8,128)S(1)}, u32[]{:S(2)}, u32[]{:S(2)}) %all-to-all-start.5) | async-done | bytes 524320 | tf_op jit(solution)/shard_map/all_to_all | solution.py:12
  136.5 1.9 fusion.44
  139.3 0.9 pad_maximum_fusion.2
  140.2 4.1 %all-to-all-start.6 = ((f32[32,40,128]{2,1,0:T(8,128)}), f32[32,40,128]{2,1,0:T(8,128)S(1)}, u32[]{:S(2)}, u32[]{:S(2)}) async-start(f32[32,40,128]{2,1,0:T(8,128)} %pad_maximum_fusion.2), calls=%async_computation.6 | async-start | bytes 1310720 | tf_op jit(solution)/shard_map/all_to_all | solution.py:12
  145.0 3.5 %fusion.71 = f32[8,32,128]{2,1,0:T(8,128)S(1)} fusion(f32[32,8,6,128]{3,0,2,1:T(8,128)S(1)} %bitcast.425, f32[2,8,8,128,128]{4,3,2,1,0:T(8,128)} %param.24), kind=kOutput, calls=%fused_computation.98 | convolution fusion | flops 150994944 | bytes 4063232 | tf_op jit(solution)/shard_map/tbkc,bkrc->tbr/dot_general | solution.py:66
  148.6 8.2 %all-to-all-done.6 = f32[32,40,128]{2,1,0:T(8,128)S(1)} async-done(((f32[32,40,128]{2,1,0:T(8,128)}), f32[32,40,128]{2,1,0:T(8,128)S(1)}, u32[]{:S(2)}, u32[]{:S(2)}) %all-to-all-start.6) | async-done | bytes 655392 | tf_op jit(solution)/shard_map/all_to_all | solution.py:12
  157.5 1.9 fusion.45
  159.5 7.3 %collective-permute-done.2 = f32[32,1024]{1,0:T(8,128)S(1)} collective-permute-done((f32[32,1024]{1,0:T(8,128)S(1)}, f32[32,1024]{1,0:T(8,128)S(1)}, u32[]{:S(2)}, u32[]{:S(2)}) %collective-permute-start.2) | collective-permute-done | bytes 131104 | tf_op jit(solution)/shard_map/ppermute | solution.py:100
  168.0 0.9 broadcast_select_fusion.13
  168.9 3.9 %all-to-all-start.7 = ((f32[32,32,128]{2,1,0:T(8,128)}), f32[32,32,128]{2,1,0:T(8,128)S(1)}, u32[]{:S(2)}, u32[]{:S(2)}) async-start(f32[32,32,128]{2,1,0:T(8,128)} %broadcast_select_fusion.13), calls=%async_computation.7 | async-start | bytes 1048576 | tf_op jit(solution)/shard_map/all_to_all | solution.py:12
  172.9 3.5 %fusion.59 = f32[8,32,128]{2,1,0:T(8,128)S(1)} fusion(f32[32,8,6,128]{3,0,2,1:T(8,128)S(1)} %bitcast.426, f32[2,8,8,128,128]{4,3,2,1,0:T(8,128)} %param.24), kind=kOutput, calls=%fused_computation.94 | convolution fusion | flops 150994944 | bytes 4063232 | tf_op jit(solution)/shard_map/tbkc,bkrc->tbr/dot_general | solution.py:66
  176.5 7.4 %all-to-all-done.7 = f32[32,32,128]{2,1,0:T(8,128)S(1)} async-done(((f32[32,32,128]{2,1,0:T(8,128)}), f32[32,32,128]{2,1,0:T(8,128)S(1)}, u32[]{:S(2)}, u32[]{:S(2)}) %all-to-all-start.7) | async-done | bytes 524320 | tf_op jit(solution)/shard_map/all_to_all | solution.py:12
  184.5 1.9 fusion.46
  187.3 0.9 pad_maximum_fusion.3
  188.2 4.3 %all-to-all-start.8 = ((f32[32,40,128]{2,1,0:T(8,128)}), f32[32,40,128]{2,1,0:T(8,128)S(1)}, u32[]{:S(2)}, u32[]{:S(2)}) async-start(f32[32,40,128]{2,1,0:T(8,128)} %pad_maximum_fusion.3), calls=%async_computation.8 | async-start | bytes 1310720 | tf_op jit(solution)/shard_map/all_to_all | solution.py:12
  193.2 3.5 %fusion.74 = f32[8,32,128]{2,1,0:T(8,128)S(1)} fusion(f32[32,8,6,128]{3,0,2,1:T(8,128)S(1)} %bitcast.427, f32[2,8,8,128,128]{4,3,2,1,0:T(8,128)} %param.24), kind=kOutput, calls=%fused_computation.99 | convolution fusion | flops 150994944 | bytes 4063232 | tf_op jit(solution)/shard_map/tbkc,bkrc->tbr/dot_general | solution.py:66
  196.8 8.0 %all-to-all-done.8 = f32[32,40,128]{2,1,0:T(8,128)S(1)} async-done(((f32[32,40,128]{2,1,0:T(8,128)}), f32[32,40,128]{2,1,0:T(8,128)S(1)}, u32[]{:S(2)}, u32[]{:S(2)}) %all-to-all-start.8) | async-done | bytes 655392 | tf_op jit(solution)/shard_map/all_to_all | solution.py:12
  205.6 1.9 fusion.47
  207.6 7.3 %collective-permute-done.3 = f32[32,1024]{1,0:T(8,128)S(1)} collective-permute-done((f32[32,1024]{1,0:T(8,128)S(1)}, f32[32,1024]{1,0:T(8,128)S(1)}, u32[]{:S(2)}, u32[]{:S(2)}) %collective-permute-start.3) | collective-permute-done | bytes 131104 | tf_op jit(solution)/shard_map/ppermute | solution.py:100
  216.1 0.9 broadcast_select_fusion.11
  217.0 3.9 %all-to-all-start.9 = ((f32[32,32,128]{2,1,0:T(8,128)}), f32[32,32,128]{2,1,0:T(8,128)S(1)}, u32[]{:S(2)}, u32[]{:S(2)}) async-start(f32[32,32,128]{2,1,0:T(8,128)} %broadcast_select_fusion.11), calls=%async_computation.9 | async-start | bytes 1048576 | tf_op jit(solution)/shard_map/all_to_all | solution.py:12
  221.0 3.5 %fusion.62 = f32[8,32,128]{2,1,0:T(8,128)S(1)} fusion(f32[32,8,6,128]{3,0,2,1:T(8,128)S(1)} %bitcast.418, f32[2,8,8,128,128]{4,3,2,1,0:T(8,128)} %param.24), kind=kOutput, calls=%fused_computation.95 | convolution fusion | flops 150994944 | bytes 4063232 | tf_op jit(solution)/shard_map/tbkc,bkrc->tbr/dot_general | solution.py:66
  224.6 7.4 %all-to-all-done.9 = f32[32,32,128]{2,1,0:T(8,128)S(1)} async-done(((f32[32,32,128]{2,1,0:T(8,128)}), f32[32,32,128]{2,1,0:T(8,128)S(1)}, u32[]{:S(2)}, u32[]{:S(2)}) %all-to-all-start.9) | async-done | bytes 524320 | tf_op jit(solution)/shard_map/all_to_all | solution.py:12
  232.6 1.9 fusion.48
  235.4 0.9 pad_maximum_fusion.4
  236.3 4.1 %all-to-all-start.10 = ((f32[32,40,128]{2,1,0:T(8,128)}), f32[32,40,128]{2,1,0:T(8,128)S(1)}, u32[]{:S(2)}, u32[]{:S(2)}) async-start(f32[32,40,128]{2,1,0:T(8,128)} %pad_maximum_fusion.4), calls=%async_computation.10 | async-start | bytes 1310720 | tf_op jit(solution)/shard_map/all_to_all | solution.py:12
  240.4 1.3 collective-permute-start.6
  241.7 0.7 collective-permute-start.5
  243.1 3.5 %fusion.77 = f32[8,32,128]{2,1,0:T(8,128)S(1)} fusion(f32[32,8,6,128]{3,0,2,1:T(8,128)S(1)} %bitcast.419, f32[2,8,8,128,128]{4,3,2,1,0:T(8,128)} %param.24), kind=kOutput, calls=%fused_computation.100 | convolution fusion | flops 150994944 | bytes 4063232 | tf_op jit(solution)/shard_map/tbkc,bkrc->tbr/dot_general | solution.py:66
  246.7 6.3 %all-to-all-done.10 = f32[32,40,128]{2,1,0:T(8,128)S(1)} async-done(((f32[32,40,128]{2,1,0:T(8,128)}), f32[32,40,128]{2,1,0:T(8,128)S(1)}, u32[]{:S(2)}, u32[]{:S(2)}) %all-to-all-start.10) | async-done | bytes 655392 | tf_op jit(solution)/shard_map/all_to_all | solution.py:12
  253.8 1.9 fusion.49
  255.7 0.7 collective-permute-start.4
  256.4 0.6 slice_select_fusion.2
  (156 shorter events, 25.0 us)
Async XLA Ops:
  0.0 28.9 %copy-start.1 = (f32[2,1024]{1,0:T(2,128)S(1)}, f32[2,1024]{1,0:T(2,128)}, u32[]{:S(2)}) copy-start(f32[2,1024]{1,0:T(2,128)} %param.23) | copy-start | bytes 24580
  1.4 41.0 %copy-start = (f32[64,1024]{1,0:T(8,128)S(1)}, f32[64,1024]{1,0:T(8,128)}, u32[]{:S(2)}) copy-start(f32[64,1024]{1,0:T(8,128)} %param.21) | copy-start | bytes 786436
  4.9 15.9 %all-to-all-start = ((f32[32,1,130]{2,1,0:T(1,128)}), f32[32,1,130]{2,1,0:T(1,128)S(1)}, u32[]{:S(2)}, u32[]{:S(2)}) async-start(f32[32,1,130]{2,1,0:T(1,128)} %all_to_all.38), calls=%async_computation | async-start | bytes 65536 | tf_op jit(solution)/shard_map/all_to_all | solution.py:12
  22.8 17.0 %all-to-all-start.1 = ((f32[32,32,128]{2,1,0:T(8,128)}), f32[32,32,128]{2,1,0:T(8,128)S(1)}, u32[]{:S(2)}, u32[]{:S(2)}) async-start(f32[32,32,128]{2,1,0:T(8,128)} %broadcast_select_fusion.19), calls=%async_computation.1 | async-start | bytes 1048576 | tf_op jit(solution)/shard_map/all_to_all | solution.py:12
  44.2 16.7 %all-to-all-start.2 = ((f32[32,40,128]{2,1,0:T(8,128)}), f32[32,40,128]{2,1,0:T(8,128)S(1)}, u32[]{:S(2)}, u32[]{:S(2)}) async-start(f32[32,40,128]{2,1,0:T(8,128)} %pad_maximum_fusion), calls=%async_computation.2 | async-start | bytes 1310720 | tf_op jit(solution)/shard_map/all_to_all | solution.py:12
  63.5 7.3 %collective-permute-start = (f32[32,1024]{1,0:T(8,128)S(1)}, f32[32,1024]{1,0:T(8,128)S(1)}, u32[]{:S(2)}, u32[]{:S(2)}) collective-permute-start(f32[32,1024]{1,0:T(8,128)S(1)} %bitcast_add_fusion.8), channel_id=1, source_target_pairs={{0,32},{32,64},{64,96},{96,0},{1,33},{33,65},{65,97},{97,1},{2,34}... | collective-permute-start | bytes 393224 | tf_op jit(solution)/shard_map/ppermute | solution.py:100
  72.9 15.0 %all-to-all-start.3 = ((f32[32,32,128]{2,1,0:T(8,128)}), f32[32,32,128]{2,1,0:T(8,128)S(1)}, u32[]{:S(2)}, u32[]{:S(2)}) async-start(f32[32,32,128]{2,1,0:T(8,128)} %broadcast_select_fusion.17), calls=%async_computation.3 | async-start | bytes 1048576 | tf_op jit(solution)/shard_map/all_to_all | solution.py:12
  92.2 16.6 %all-to-all-start.4 = ((f32[32,40,128]{2,1,0:T(8,128)}), f32[32,40,128]{2,1,0:T(8,128)S(1)}, u32[]{:S(2)}, u32[]{:S(2)}) async-start(f32[32,40,128]{2,1,0:T(8,128)} %pad_maximum_fusion.1), calls=%async_computation.4 | async-start | bytes 1310720 | tf_op jit(solution)/shard_map/all_to_all | solution.py:12
  111.4 7.3 %collective-permute-start.1 = (f32[32,1024]{1,0:T(8,128)S(1)}, f32[32,1024]{1,0:T(8,128)S(1)}, u32[]{:S(2)}, u32[]{:S(2)}) collective-permute-start(f32[32,1024]{1,0:T(8,128)S(1)} %bitcast_add_fusion.6), channel_id=1, source_target_pairs={{0,32},{32,64},{64,96},{96,0},{1,33},{33,65},{65,97},{97,1},{2,34}... | collective-permute-start | bytes 393224 | tf_op jit(solution)/shard_map/ppermute | solution.py:100
  120.9 15.0 %all-to-all-start.5 = ((f32[32,32,128]{2,1,0:T(8,128)}), f32[32,32,128]{2,1,0:T(8,128)S(1)}, u32[]{:S(2)}, u32[]{:S(2)}) async-start(f32[32,32,128]{2,1,0:T(8,128)} %broadcast_select_fusion.15), calls=%async_computation.5 | async-start | bytes 1048576 | tf_op jit(solution)/shard_map/all_to_all | solution.py:12
  140.2 16.6 %all-to-all-start.6 = ((f32[32,40,128]{2,1,0:T(8,128)}), f32[32,40,128]{2,1,0:T(8,128)S(1)}, u32[]{:S(2)}, u32[]{:S(2)}) async-start(f32[32,40,128]{2,1,0:T(8,128)} %pad_maximum_fusion.2), calls=%async_computation.6 | async-start | bytes 1310720 | tf_op jit(solution)/shard_map/all_to_all | solution.py:12
  159.4 7.3 %collective-permute-start.2 = (f32[32,1024]{1,0:T(8,128)S(1)}, f32[32,1024]{1,0:T(8,128)S(1)}, u32[]{:S(2)}, u32[]{:S(2)}) collective-permute-start(f32[32,1024]{1,0:T(8,128)S(1)} %bitcast_add_fusion.4), channel_id=1, source_target_pairs={{0,32},{32,64},{64,96},{96,0},{1,33},{33,65},{65,97},{97,1},{2,34}... | collective-permute-start | bytes 393224 | tf_op jit(solution)/shard_map/ppermute | solution.py:100
  168.9 15.0 %all-to-all-start.7 = ((f32[32,32,128]{2,1,0:T(8,128)}), f32[32,32,128]{2,1,0:T(8,128)S(1)}, u32[]{:S(2)}, u32[]{:S(2)}) async-start(f32[32,32,128]{2,1,0:T(8,128)} %broadcast_select_fusion.13), calls=%async_computation.7 | async-start | bytes 1048576 | tf_op jit(solution)/shard_map/all_to_all | solution.py:12
  184.4 21.2 %copy-start.2 = (f32[64]{0:T(128)S(1)}, f32[64]{0:T(128)}, u32[]{:S(2)}) copy-start(f32[64]{0:T(128)} %param.22) | copy-start | bytes 772
  188.2 16.7 %all-to-all-start.8 = ((f32[32,40,128]{2,1,0:T(8,128)}), f32[32,40,128]{2,1,0:T(8,128)S(1)}, u32[]{:S(2)}, u32[]{:S(2)}) async-start(f32[32,40,128]{2,1,0:T(8,128)} %pad_maximum_fusion.3), calls=%async_computation.8 | async-start | bytes 1310720 | tf_op jit(solution)/shard_map/all_to_all | solution.py:12
  207.6 7.3 %collective-permute-start.3 = (f32[32,1024]{1,0:T(8,128)S(1)}, f32[32,1024]{1,0:T(8,128)S(1)}, u32[]{:S(2)}, u32[]{:S(2)}) collective-permute-start(f32[32,1024]{1,0:T(8,128)S(1)} %get-tuple-element.71), channel_id=1, source_target_pairs={{0,32},{32,64},{64,96},{96,0},{1,33},{33,65},{65,97},{97,1},{2,34}... | collective-permute-start | bytes 393224 | tf_op jit(solution)/shard_map/ppermute | solution.py:100
  217.0 15.0 %all-to-all-start.9 = ((f32[32,32,128]{2,1,0:T(8,128)}), f32[32,32,128]{2,1,0:T(8,128)S(1)}, u32[]{:S(2)}, u32[]{:S(2)}) async-start(f32[32,32,128]{2,1,0:T(8,128)} %broadcast_select_fusion.11), calls=%async_computation.9 | async-start | bytes 1048576 | tf_op jit(solution)/shard_map/all_to_all | solution.py:12
  236.3 16.7 %all-to-all-start.10 = ((f32[32,40,128]{2,1,0:T(8,128)}), f32[32,40,128]{2,1,0:T(8,128)S(1)}, u32[]{:S(2)}, u32[]{:S(2)}) async-start(f32[32,40,128]{2,1,0:T(8,128)} %pad_maximum_fusion.4), calls=%async_computation.10 | async-start | bytes 1310720 | tf_op jit(solution)/shard_map/all_to_all | solution.py:12
  240.4 16.0 %collective-permute-start.6 = (f32[16,1024]{1,0:T(8,128)S(1)}, f32[16,1024]{1,0:T(8,128)S(1)}, u32[]{:S(2)}, u32[]{:S(2)}) collective-permute-start(f32[16,1024]{1,0:T(8,128)S(1)} %get-tuple-element.82), channel_id=1, source_target_pairs={{96,0},{97,1},{98,2},{99,3},{100,4},{101,5},{102,6},{103,7},{104,8... | collective-permute-start | bytes 196616 | tf_op jit(solution)/shard_map/ppermute | solution.py:97
  241.7 14.7 %collective-permute-start.5 = (f32[16,1024]{1,0:T(8,128)S(1)}, f32[16,1024]{1,0:T(8,128)S(1)}, u32[]{:S(2)}, u32[]{:S(2)}) collective-permute-start(f32[16,1024]{1,0:T(8,128)S(1)} %get-tuple-element.83), channel_id=1, source_target_pairs={{96,32},{97,33},{98,34},{99,35},{100,36},{101,37},{102,38},{103,39... | collective-permute-start | bytes 196616 | tf_op jit(solution)/shard_map/ppermute | solution.py:97
  255.7 0.7 collective-permute-start.4

commit v3 on v2

--- a/solution.py
+++ b/solution.py
@@ -16,7 +16,6 @@
     sections = lax.axis_size("month")
     devices = lax.axis_size("grid")
     section = lax.axis_index("month")
-    me = lax.axis_index("grid")
     months_here = blocks.shape[0]
     blk_count = blocks.shape[1]
     nk = blocks.shape[2]
@@ -41,28 +40,29 @@
     c_loc = jnp.sum(jnp.where(to_blk[:, :, :, None], colsum[:, :near, None, :], 0.0), axis=(0, 1))
     far_cs = colsum[:, near:].reshape(-1, blk_size)
     cs_send = jnp.sum(jnp.where(hit[last_m][:, :, None], far_cs[None], 0.0), axis=1)
-    sent = jnp.concatenate([cs_send, req.T.astype(jnp.float32)], axis=1)
-    recv = exchange(sent, "grid")
-    want = jnp.round(recv[:, blk_size:]).astype(jnp.int32)
+    want = exchange(req.T, "grid")
     send_idx = jnp.maximum(want, 0)
     from_e = want[:, last_m][:, None] == jnp.arange(blk_count, dtype=jnp.int32)[None, :]
-    c_far = jnp.sum(jnp.where(from_e[:, :, None], recv[:, None, :blk_size], 0.0), axis=0)
-    c_all = (retain[last_m].reshape(blk_count, blk_size) + c_loc + c_far).reshape(rows_here)
+    base_c = retain[last_m].reshape(blk_count, blk_size) + c_loc
 
-    def apply_month(state, j):
+    def apply_month(state, j, c_all):
         sb = state.reshape(batch, blk_count, blk_size)
-        out = jnp.take(sb, send_idx[:, j], axis=1).transpose(1, 0, 2)
+        out = jnp.take(sb, send_idx[:, j], axis=1, mode="clip").transpose(1, 0, 2)
         if j == last_m:
             part = jnp.sum(state * c_all[None, :], axis=1)
             row = jnp.zeros((devices, 8, blk_size), jnp.float32).at[:, 0, :batch].set(part[None, :])
+            row = row.at[:, 1, :].set(cs_send)
             full = exchange(jnp.concatenate([out, row], axis=1), "grid")
             inventory = jnp.sum(full[:, batch, :batch], axis=0)
             got = full[:, :batch].transpose(1, 0, 2)
+            c_far = jnp.sum(jnp.where(from_e[:, :, None], full[:, None, batch + 1, :], 0.0), axis=0)
+            c_all = (base_c + c_far).reshape(rows_here)
         else:
             inventory = None
-            got = exchange(out, "grid").transpose(1, 0, 2)
-        loc = jnp.take(sb, src_blk[j, :, :near].reshape(-1), axis=1).reshape(batch, blk_count, near, blk_size)
-        far = jnp.take(got, src_dev[j, :, near:].reshape(-1), axis=1).reshape(batch, blk_count, FAR, blk_size)
+            got = exchange(out, "grid")
+            got = got.transpose(1, 0, 2)
+        loc = jnp.take(sb, src_blk[j, :, :near].reshape(-1), axis=1, mode="clip").reshape(batch, blk_count, near, blk_size)
+        far = jnp.take(got, src_dev[j, :, near:].reshape(-1), axis=1, mode="clip").reshape(batch, blk_count, FAR, blk_size)
         mixed = jnp.einsum(
             "tbkc,bkrc->tbr",
             loc,
@@ -76,9 +76,10 @@
             precision=PRECISION,
             preferred_element_type=jnp.float32,
         )
-        return retain[j][None, :] * state + mixed.reshape(batch, rows_here), inventory
+        return retain[j][None, :] * state + mixed.reshape(batch, rows_here), inventory, c_all
 
     held = jnp.zeros((batch, rows_here), jnp.float32)
+    c_all = jnp.zeros((rows_here,), jnp.float32)
     result = jnp.zeros((own, rows_here), jnp.float32)
     last = sections - 1
     steps = NBATCH + sections - 1
@@ -86,7 +87,7 @@
         if step < NBATCH:
             held = jnp.where(section == 0, tracers[step * batch : (step + 1) * batch], held)
         for j in range(months_here):
-            held, inventory = apply_month(held, j)
+            held, inventory, c_all = apply_month(held, j, c_all)
         b = step - last
         if b >= 0:
             scaled = held * (targets[b * batch : (b + 1) * batch] * points / inventory)[:, None]

time: 261 us -> 252 us (0.966)
  other arithmetic: 18.5 us -> 11.6 us
  waiting for transfers between devices: 108 us -> 103 us
  local copies, waits for them, and re-layouts: 19.9 us -> 24.7 us
    select_n x36 -> x0, other arithmetic: 7.08 us -> none  [the longest x12 5 us: apply_month(): out = jnp.take(sb, send_idx[:, j], axis=1).transpose(1, 0, 2)]
    all_to_all x11, waiting for transfers between devices: 80.8 us -> 75.9 us  [exchange(): return lax.all_to_all(x, axis, 0, 0, tiled=True)]
    gather x30, local copies, waits for them, and re-layouts: 17.6 us -> 21.6 us  [the longest x10 9.81 us: apply_month(): out = jnp.take(sb, send_idx[:, j], axis=1, mode='clip').transpose(1, 0, 2)]
  transfers between devices with their start and end apart: 18 -> 18, of which waited for: 15 -> 15; matrix products, arithmetic and copies ran while one was open for 17% -> 20% of each run, Pallas kernels for 0% -> 0%
where the time goes in v3:
time: 252 us; the launch traced here: 248 us
  waiting for transfers between devices  103 us (41%)
  starting transfers between devices  54.2 us (22%)
  matrix products  53.6 us (21%)
  local copies, waits for them, and re-layouts  24.7 us (10%)
  other arithmetic  11.6 us (5%)
    all_to_all x11, waiting for transfers between devices, exchange(): return lax.all_to_all(x, axis, 0, 0, tiled=True)  75.9 us
    all_to_all x11, starting transfers between devices, exchange(): return lax.all_to_all(x, axis, 0, 0, tiled=True)  49.3 us
    dot_general x10, matrix products, apply_month(): jnp.einsum('tbkc,bkrc->tbr', loc, blocks[j, :, :near], precision=PRECISIO...  35.1 us
    ppermute x4, waiting for transfers between devices, local(): lax.ppermute(held, 'month', [(i, (i + 1) % sections) for i in range(secti...  27.3 us
    dot_general x10, matrix products, apply_month(): jnp.einsum('tbkc,bkrc->tbr', far, blocks[j, :, near:], precision=PRECISIO...  18.5 us
    gather x10, local copies, waits for them, and re-layouts, apply_month(): out = jnp.take(sb, send_idx[:, j], axis=1, mode='clip').transpose(1, 0, 2)  9.81 us
    gather x10, local copies, waits for them, and re-layouts, apply_month(): jnp.take(sb, src_blk[j, :, :near].reshape(-1), axis=1, mode='clip')  6.09 us
    gather x10, local copies, waits for them, and re-layouts, apply_month(): jnp.take(got, src_dev[j, :, near:].reshape(-1), axis=1, mode='clip')  5.67 us
  transfers between devices with their start and end apart: 18, of which 15 were waited for; matrix products, arithmetic and copies ran while one was open for 20% of the time, Pallas kernels for 0%

profile of v3, /device:TPU:0, one launch (start us, length us, event | category | flops | bytes accessed | tf_op | source)
XLA Modules:
  0.0 248.3 jit_solution(9084509943516783036)
XLA Ops:
  0.0 0.8 add_select_fusion
  1.2 0.7 copy.99
  1.9 8.4 %all-to-all-start = ((s32[32,1,2]{2,1,0:T(1,128)}), s32[32,1,2]{2,1,0:T(1,128)S(1)}, u32[]{:S(2)}, u32[]{:S(2)}) async-start(s32[32,1,2]{2,1,0:T(1,128)} %copy.99), calls=%async_computation | async-start | bytes 32768 | tf_op jit(solution)/shard_map/all_to_all | solution.py:12
  10.9 2.6 %slice_reduce_fusion = f32[8,8,128]{2,1,0:T(8,128)S(1)} fusion(f32[2,8,8,128,128]{4,3,2,1,0:T(8,128)} %param.28), kind=kLoop, calls=%fused_computation.30 | loop fusion | flops 1040384 | bytes 4227072 | tf_op jit(solution)/shard_map/reduce_sum | solution.py:38
  13.8 0.9 copy_bitcast_fusion.9
  14.8 2.9 %all-to-all-done = s32[32,1,2]{2,1,0:T(1,128)S(1)} async-done(((s32[32,1,2]{2,1,0:T(1,128)}), s32[32,1,2]{2,1,0:T(1,128)S(1)}, u32[]{:S(2)}, u32[]{:S(2)}) %all-to-all-start) | async-done | bytes 288 | tf_op jit(solution)/shard_map/all_to_all | solution.py:12
  17.7 1.4 gather_fusion.1
  19.1 4.5 %all-to-all-start.1 = ((f32[32,32,128]{2,1,0:T(8,128)}), f32[32,32,128]{2,1,0:T(8,128)S(1)}, u32[]{:S(2)}, u32[]{:S(2)}) async-start(f32[32,32,128]{2,1,0:T(8,128)} %gather_fusion.1), calls=%async_computation.1 | async-start | bytes 1048576 | tf_op jit(solution)/shard_map/all_to_all | solution.py:12
  23.7 0.7 slice.382
  25.1 3.5 %fusion.50 = f32[8,32,128]{2,1,0:T(8,128)S(1)} fusion(f32[32,8,6,128]{3,0,2,1:T(8,128)S(1)} %bitcast.406, f32[2,8,8,128,128]{4,3,2,1,0:T(8,128)} %param.28), kind=kOutput, calls=%fused_computation.91 | convolution fusion | flops 150994944 | bytes 4063232 | tf_op jit(solution)/shard_map/tbkc,bkrc->tbr/dot_general | solution.py:66
  28.6 6.1 %all-to-all-done.1 = f32[32,32,128]{2,1,0:T(8,128)S(1)} async-done(((f32[32,32,128]{2,1,0:T(8,128)}), f32[32,32,128]{2,1,0:T(8,128)S(1)}, u32[]{:S(2)}, u32[]{:S(2)}) %all-to-all-start.1) | async-done | bytes 524320 | tf_op jit(solution)/shard_map/all_to_all | solution.py:12
  35.3 1.9 fusion.40
  38.0 0.9 pad_maximum_fusion
  38.9 4.1 %all-to-all-start.2 = ((f32[32,40,128]{2,1,0:T(8,128)}), f32[32,40,128]{2,1,0:T(8,128)S(1)}, u32[]{:S(2)}, u32[]{:S(2)}) async-start(f32[32,40,128]{2,1,0:T(8,128)} %pad_maximum_fusion), calls=%async_computation.2 | async-start | bytes 1310720 | tf_op jit(solution)/shard_map/all_to_all | solution.py:12
  43.7 3.5 %fusion.65 = f32[8,32,128]{2,1,0:T(8,128)S(1)} fusion(f32[32,8,6,128]{3,0,2,1:T(8,128)S(1)} %bitcast.409, f32[2,8,8,128,128]{4,3,2,1,0:T(8,128)} %param.28), kind=kOutput, calls=%fused_computation.96 | convolution fusion | flops 150994944 | bytes 4063232 | tf_op jit(solution)/shard_map/tbkc,bkrc->tbr/dot_general | solution.py:66
  47.3 8.3 %all-to-all-done.2 = f32[32,40,128]{2,1,0:T(8,128)S(1)} async-done(((f32[32,40,128]{2,1,0:T(8,128)}), f32[32,40,128]{2,1,0:T(8,128)S(1)}, u32[]{:S(2)}, u32[]{:S(2)}) %all-to-all-start.2) | async-done | bytes 655392 | tf_op jit(solution)/shard_map/all_to_all | solution.py:12
  56.4 1.9 fusion.41
  58.3 1.6 collective-permute-start
  59.8 5.8 %collective-permute-done = f32[32,1024]{1,0:T(8,128)S(1)} collective-permute-done((f32[32,1024]{1,0:T(8,128)S(1)}, f32[32,1024]{1,0:T(8,128)S(1)}, u32[]{:S(2)}, u32[]{:S(2)}) %collective-permute-start) | collective-permute-done | bytes 131104 | tf_op jit(solution)/shard_map/ppermute | solution.py:101
  65.6 1.4 gather_fusion.7
  67.0 3.9 %all-to-all-start.3 = ((f32[32,32,128]{2,1,0:T(8,128)}), f32[32,32,128]{2,1,0:T(8,128)S(1)}, u32[]{:S(2)}, u32[]{:S(2)}) async-start(f32[32,32,128]{2,1,0:T(8,128)} %gather_fusion.7), calls=%async_computation.3 | async-start | bytes 1048576 | tf_op jit(solution)/shard_map/all_to_all | solution.py:12
  71.5 3.5 %fusion.53 = f32[8,32,128]{2,1,0:T(8,128)S(1)} fusion(f32[32,8,6,128]{3,0,2,1:T(8,128)S(1)} %bitcast.410, f32[2,8,8,128,128]{4,3,2,1,0:T(8,128)} %param.28), kind=kOutput, calls=%fused_computation.92 | convolution fusion | flops 150994944 | bytes 4063232 | tf_op jit(solution)/shard_map/tbkc,bkrc->tbr/dot_general | solution.py:66
  75.0 6.9 %all-to-all-done.3 = f32[32,32,128]{2,1,0:T(8,128)S(1)} async-done(((f32[32,32,128]{2,1,0:T(8,128)}), f32[32,32,128]{2,1,0:T(8,128)S(1)}, u32[]{:S(2)}, u32[]{:S(2)}) %all-to-all-start.3) | async-done | bytes 524320 | tf_op jit(solution)/shard_map/all_to_all | solution.py:12
  82.5 1.9 fusion.42
  85.3 0.9 pad_maximum_fusion.1
  86.1 4.1 %all-to-all-start.4 = ((f32[32,40,128]{2,1,0:T(8,128)}), f32[32,40,128]{2,1,0:T(8,128)S(1)}, u32[]{:S(2)}, u32[]{:S(2)}) async-start(f32[32,40,128]{2,1,0:T(8,128)} %pad_maximum_fusion.1), calls=%async_computation.4 | async-start | bytes 1310720 | tf_op jit(solution)/shard_map/all_to_all | solution.py:12
  90.9 3.5 %fusion.68 = f32[8,32,128]{2,1,0:T(8,128)S(1)} fusion(f32[32,8,6,128]{3,0,2,1:T(8,128)S(1)} %bitcast.411, f32[2,8,8,128,128]{4,3,2,1,0:T(8,128)} %param.28), kind=kOutput, calls=%fused_computation.97 | convolution fusion | flops 150994944 | bytes 4063232 | tf_op jit(solution)/shard_map/tbkc,bkrc->tbr/dot_general | solution.py:66
  94.4 8.4 %all-to-all-done.4 = f32[32,40,128]{2,1,0:T(8,128)S(1)} async-done(((f32[32,40,128]{2,1,0:T(8,128)}), f32[32,40,128]{2,1,0:T(8,128)S(1)}, u32[]{:S(2)}, u32[]{:S(2)}) %all-to-all-start.4) | async-done | bytes 655392 | tf_op jit(solution)/shard_map/all_to_all | solution.py:12
  103.4 1.9 fusion.43
  105.9 7.0 %collective-permute-done.1 = f32[32,1024]{1,0:T(8,128)S(1)} collective-permute-done((f32[32,1024]{1,0:T(8,128)S(1)}, f32[32,1024]{1,0:T(8,128)S(1)}, u32[]{:S(2)}, u32[]{:S(2)}) %collective-permute-start.1) | collective-permute-done | bytes 131104 | tf_op jit(solution)/shard_map/ppermute | solution.py:101
  112.8 1.4 gather_fusion.13
  114.2 3.9 %all-to-all-start.5 = ((f32[32,32,128]{2,1,0:T(8,128)}), f32[32,32,128]{2,1,0:T(8,128)S(1)}, u32[]{:S(2)}, u32[]{:S(2)}) async-start(f32[32,32,128]{2,1,0:T(8,128)} %gather_fusion.13), calls=%async_computation.5 | async-start | bytes 1048576 | tf_op jit(solution)/shard_map/all_to_all | solution.py:12
  118.9 3.5 %fusion.56 = f32[8,32,128]{2,1,0:T(8,128)S(1)} fusion(f32[32,8,6,128]{3,0,2,1:T(8,128)S(1)} %bitcast.412, f32[2,8,8,128,128]{4,3,2,1,0:T(8,128)} %param.28), kind=kOutput, calls=%fused_computation.93 | convolution fusion | flops 150994944 | bytes 4063232 | tf_op jit(solution)/shard_map/tbkc,bkrc->tbr/dot_general | solution.py:66
  122.4 6.8 %all-to-all-done.5 = f32[32,32,128]{2,1,0:T(8,128)S(1)} async-done(((f32[32,32,128]{2,1,0:T(8,128)}), f32[32,32,128]{2,1,0:T(8,128)S(1)}, u32[]{:S(2)}, u32[]{:S(2)}) %all-to-all-start.5) | async-done | bytes 524320 | tf_op jit(solution)/shard_map/all_to_all | solution.py:12
  129.8 1.9 fusion.44
  132.5 0.9 pad_maximum_fusion.2
  133.4 4.1 %all-to-all-start.6 = ((f32[32,40,128]{2,1,0:T(8,128)}), f32[32,40,128]{2,1,0:T(8,128)S(1)}, u32[]{:S(2)}, u32[]{:S(2)}) async-start(f32[32,40,128]{2,1,0:T(8,128)} %pad_maximum_fusion.2), calls=%async_computation.6 | async-start | bytes 1310720 | tf_op jit(solution)/shard_map/all_to_all | solution.py:12
  138.1 3.5 %fusion.71 = f32[8,32,128]{2,1,0:T(8,128)S(1)} fusion(f32[32,8,6,128]{3,0,2,1:T(8,128)S(1)} %bitcast.413, f32[2,8,8,128,128]{4,3,2,1,0:T(8,128)} %param.28), kind=kOutput, calls=%fused_computation.98 | convolution fusion | flops 150994944 | bytes 4063232 | tf_op jit(solution)/shard_map/tbkc,bkrc->tbr/dot_general | solution.py:66
  141.6 8.4 %all-to-all-done.6 = f32[32,40,128]{2,1,0:T(8,128)S(1)} async-done(((f32[32,40,128]{2,1,0:T(8,128)}), f32[32,40,128]{2,1,0:T(8,128)S(1)}, u32[]{:S(2)}, u32[]{:S(2)}) %all-to-all-start.6) | async-done | bytes 655392 | tf_op jit(solution)/shard_map/all_to_all | solution.py:12
  150.6 1.9 fusion.45
  152.6 7.2 %collective-permute-done.2 = f32[32,1024]{1,0:T(8,128)S(1)} collective-permute-done((f32[32,1024]{1,0:T(8,128)S(1)}, f32[32,1024]{1,0:T(8,128)S(1)}, u32[]{:S(2)}, u32[]{:S(2)}) %collective-permute-start.2) | collective-permute-done | bytes 131104 | tf_op jit(solution)/shard_map/ppermute | solution.py:101
  159.9 1.4 gather_fusion.19
  161.3 3.9 %all-to-all-start.7 = ((f32[32,32,128]{2,1,0:T(8,128)}), f32[32,32,128]{2,1,0:T(8,128)S(1)}, u32[]{:S(2)}, u32[]{:S(2)}) async-start(f32[32,32,128]{2,1,0:T(8,128)} %gather_fusion.19), calls=%async_computation.7 | async-start | bytes 1048576 | tf_op jit(solution)/shard_map/all_to_all | solution.py:12
  165.9 3.5 %fusion.59 = f32[8,32,128]{2,1,0:T(8,128)S(1)} fusion(f32[32,8,6,128]{3,0,2,1:T(8,128)S(1)} %bitcast.414, f32[2,8,8,128,128]{4,3,2,1,0:T(8,128)} %param.28), kind=kOutput, calls=%fused_computation.94 | convolution fusion | flops 150994944 | bytes 4063232 | tf_op jit(solution)/shard_map/tbkc,bkrc->tbr/dot_general | solution.py:66
  169.4 6.8 %all-to-all-done.7 = f32[32,32,128]{2,1,0:T(8,128)S(1)} async-done(((f32[32,32,128]{2,1,0:T(8,128)}), f32[32,32,128]{2,1,0:T(8,128)S(1)}, u32[]{:S(2)}, u32[]{:S(2)}) %all-to-all-start.7) | async-done | bytes 524320 | tf_op jit(solution)/shard_map/all_to_all | solution.py:12
  176.8 1.9 fusion.46
  179.5 0.9 pad_maximum_fusion.3
  180.4 4.1 %all-to-all-start.8 = ((f32[32,40,128]{2,1,0:T(8,128)}), f32[32,40,128]{2,1,0:T(8,128)S(1)}, u32[]{:S(2)}, u32[]{:S(2)}) async-start(f32[32,40,128]{2,1,0:T(8,128)} %pad_maximum_fusion.3), calls=%async_computation.8 | async-start | bytes 1310720 | tf_op jit(solution)/shard_map/all_to_all | solution.py:12
  185.1 3.5 %fusion.74 = f32[8,32,128]{2,1,0:T(8,128)S(1)} fusion(f32[32,8,6,128]{3,0,2,1:T(8,128)S(1)} %bitcast.415, f32[2,8,8,128,128]{4,3,2,1,0:T(8,128)} %param.28), kind=kOutput, calls=%fused_computation.99 | convolution fusion | flops 150994944 | bytes 4063232 | tf_op jit(solution)/shard_map/tbkc,bkrc->tbr/dot_general | solution.py:66
  188.6 8.4 %all-to-all-done.8 = f32[32,40,128]{2,1,0:T(8,128)S(1)} async-done(((f32[32,40,128]{2,1,0:T(8,128)}), f32[32,40,128]{2,1,0:T(8,128)S(1)}, u32[]{:S(2)}, u32[]{:S(2)}) %all-to-all-start.8) | async-done | bytes 655392 | tf_op jit(solution)/shard_map/all_to_all | solution.py:12
  197.7 1.9 fusion.47
  199.8 7.3 %collective-permute-done.3 = f32[32,1024]{1,0:T(8,128)S(1)} collective-permute-done((f32[32,1024]{1,0:T(8,128)S(1)}, f32[32,1024]{1,0:T(8,128)S(1)}, u32[]{:S(2)}, u32[]{:S(2)}) %collective-permute-start.3) | collective-permute-done | bytes 131104 | tf_op jit(solution)/shard_map/ppermute | solution.py:101
  207.0 1.4 gather_fusion.25
  208.4 4.1 %all-to-all-start.9 = ((f32[32,32,128]{2,1,0:T(8,128)}), f32[32,32,128]{2,1,0:T(8,128)S(1)}, u32[]{:S(2)}, u32[]{:S(2)}) async-start(f32[32,32,128]{2,1,0:T(8,128)} %gather_fusion.25), calls=%async_computation.9 | async-start | bytes 1048576 | tf_op jit(solution)/shard_map/all_to_all | solution.py:12
  213.3 3.5 %fusion.62 = f32[8,32,128]{2,1,0:T(8,128)S(1)} fusion(f32[32,8,6,128]{3,0,2,1:T(8,128)S(1)} %bitcast.407, f32[2,8,8,128,128]{4,3,2,1,0:T(8,128)} %param.28), kind=kOutput, calls=%fused_computation.95 | convolution fusion | flops 150994944 | bytes 4063232 | tf_op jit(solution)/shard_map/tbkc,bkrc->tbr/dot_general | solution.py:66
  216.8 6.6 %all-to-all-done.9 = f32[32,32,128]{2,1,0:T(8,128)S(1)} async-done(((f32[32,32,128]{2,1,0:T(8,128)}), f32[32,32,128]{2,1,0:T(8,128)S(1)}, u32[]{:S(2)}, u32[]{:S(2)}) %all-to-all-start.9) | async-done | bytes 524320 | tf_op jit(solution)/shard_map/all_to_all | solution.py:12
  223.9 1.9 fusion.48
  226.7 0.9 pad_maximum_fusion.4
  227.5 4.1 %all-to-all-start.10 = ((f32[32,40,128]{2,1,0:T(8,128)}), f32[32,40,128]{2,1,0:T(8,128)S(1)}, u32[]{:S(2)}, u32[]{:S(2)}) async-start(f32[32,40,128]{2,1,0:T(8,128)} %pad_maximum_fusion.4), calls=%async_computation.10 | async-start | bytes 1310720 | tf_op jit(solution)/shard_map/all_to_all | solution.py:12
  231.7 1.3 collective-permute-start.6
  233.0 0.7 collective-permute-start.5
  234.3 3.5 %fusion.77 = f32[8,32,128]{2,1,0:T(8,128)S(1)} fusion(f32[32,8,6,128]{3,0,2,1:T(8,128)S(1)} %bitcast.408, f32[2,8,8,128,128]{4,3,2,1,0:T(8,128)} %param.28), kind=kOutput, calls=%fused_computation.100 | convolution fusion | flops 150994944 | bytes 4063232 | tf_op jit(solution)/shard_map/tbkc,bkrc->tbr/dot_general | solution.py:66
  237.8 6.4 %all-to-all-done.10 = f32[32,40,128]{2,1,0:T(8,128)S(1)} async-done(((f32[32,40,128]{2,1,0:T(8,128)}), f32[32,40,128]{2,1,0:T(8,128)S(1)}, u32[]{:S(2)}, u32[]{:S(2)}) %all-to-all-start.10) | async-done | bytes 655392 | tf_op jit(solution)/shard_map/all_to_all | solution.py:12
  245.0 1.8 fusion.49
  (126 shorter events, 20.7 us)
Async XLA Ops:
  0.0 37.1 %copy-start = (f32[64,1024]{1,0:T(8,128)S(1)}, f32[64,1024]{1,0:T(8,128)}, u32[]{:S(2)}) copy-start(f32[64,1024]{1,0:T(8,128)} %param.25) | copy-start | bytes 786436
  1.9 15.8 %all-to-all-start = ((s32[32,1,2]{2,1,0:T(1,128)}), s32[32,1,2]{2,1,0:T(1,128)S(1)}, u32[]{:S(2)}, u32[]{:S(2)}) async-start(s32[32,1,2]{2,1,0:T(1,128)} %copy.99), calls=%async_computation | async-start | bytes 32768 | tf_op jit(solution)/shard_map/all_to_all | solution.py:12
  19.1 15.6 %all-to-all-start.1 = ((f32[32,32,128]{2,1,0:T(8,128)}), f32[32,32,128]{2,1,0:T(8,128)S(1)}, u32[]{:S(2)}, u32[]{:S(2)}) async-start(f32[32,32,128]{2,1,0:T(8,128)} %gather_fusion.1), calls=%async_computation.1 | async-start | bytes 1048576 | tf_op jit(solution)/shard_map/all_to_all | solution.py:12
  25.1 31.3 %copy-start.1 = (f32[2,1024]{1,0:T(2,128)S(1)}, f32[2,1024]{1,0:T(2,128)}, u32[]{:S(2)}) copy-start(f32[2,1024]{1,0:T(2,128)} %param.27) | copy-start | bytes 24580
  38.9 16.7 %all-to-all-start.2 = ((f32[32,40,128]{2,1,0:T(8,128)}), f32[32,40,128]{2,1,0:T(8,128)S(1)}, u32[]{:S(2)}, u32[]{:S(2)}) async-start(f32[32,40,128]{2,1,0:T(8,128)} %pad_maximum_fusion), calls=%async_computation.2 | async-start | bytes 1310720 | tf_op jit(solution)/shard_map/all_to_all | solution.py:12
  58.3 7.3 %collective-permute-start = (f32[32,1024]{1,0:T(8,128)S(1)}, f32[32,1024]{1,0:T(8,128)S(1)}, u32[]{:S(2)}, u32[]{:S(2)}) collective-permute-start(f32[32,1024]{1,0:T(8,128)S(1)} %bitcast_add_fusion.8), channel_id=1, source_target_pairs={{0,32},{32,64},{64,96},{96,0},{1,33},{33,65},{65,97},{97,1},{2,34}... | collective-permute-start | bytes 393224 | tf_op jit(solution)/shard_map/ppermute | solution.py:101
  67.0 15.0 %all-to-all-start.3 = ((f32[32,32,128]{2,1,0:T(8,128)}), f32[32,32,128]{2,1,0:T(8,128)S(1)}, u32[]{:S(2)}, u32[]{:S(2)}) async-start(f32[32,32,128]{2,1,0:T(8,128)} %gather_fusion.7), calls=%async_computation.3 | async-start | bytes 1048576 | tf_op jit(solution)/shard_map/all_to_all | solution.py:12
  86.1 16.6 %all-to-all-start.4 = ((f32[32,40,128]{2,1,0:T(8,128)}), f32[32,40,128]{2,1,0:T(8,128)S(1)}, u32[]{:S(2)}, u32[]{:S(2)}) async-start(f32[32,40,128]{2,1,0:T(8,128)} %pad_maximum_fusion.1), calls=%async_computation.4 | async-start | bytes 1310720 | tf_op jit(solution)/shard_map/all_to_all | solution.py:12
  105.3 7.5 %collective-permute-start.1 = (f32[32,1024]{1,0:T(8,128)S(1)}, f32[32,1024]{1,0:T(8,128)S(1)}, u32[]{:S(2)}, u32[]{:S(2)}) collective-permute-start(f32[32,1024]{1,0:T(8,128)S(1)} %bitcast_add_fusion.6), channel_id=1, source_target_pairs={{0,32},{32,64},{64,96},{96,0},{1,33},{33,65},{65,97},{97,1},{2,34}... | collective-permute-start | bytes 393224 | tf_op jit(solution)/shard_map/ppermute | solution.py:101
  114.2 15.0 %all-to-all-start.5 = ((f32[32,32,128]{2,1,0:T(8,128)}), f32[32,32,128]{2,1,0:T(8,128)S(1)}, u32[]{:S(2)}, u32[]{:S(2)}) async-start(f32[32,32,128]{2,1,0:T(8,128)} %gather_fusion.13), calls=%async_computation.5 | async-start | bytes 1048576 | tf_op jit(solution)/shard_map/all_to_all | solution.py:12
  133.4 16.6 %all-to-all-start.6 = ((f32[32,40,128]{2,1,0:T(8,128)}), f32[32,40,128]{2,1,0:T(8,128)S(1)}, u32[]{:S(2)}, u32[]{:S(2)}) async-start(f32[32,40,128]{2,1,0:T(8,128)} %pad_maximum_fusion.2), calls=%async_computation.6 | async-start | bytes 1310720 | tf_op jit(solution)/shard_map/all_to_all | solution.py:12
  152.5 7.3 %collective-permute-start.2 = (f32[32,1024]{1,0:T(8,128)S(1)}, f32[32,1024]{1,0:T(8,128)S(1)}, u32[]{:S(2)}, u32[]{:S(2)}) collective-permute-start(f32[32,1024]{1,0:T(8,128)S(1)} %bitcast_add_fusion.4), channel_id=1, source_target_pairs={{0,32},{32,64},{64,96},{96,0},{1,33},{33,65},{65,97},{97,1},{2,34}... | collective-permute-start | bytes 393224 | tf_op jit(solution)/shard_map/ppermute | solution.py:101
  161.3 15.0 %all-to-all-start.7 = ((f32[32,32,128]{2,1,0:T(8,128)}), f32[32,32,128]{2,1,0:T(8,128)S(1)}, u32[]{:S(2)}, u32[]{:S(2)}) async-start(f32[32,32,128]{2,1,0:T(8,128)} %gather_fusion.19), calls=%async_computation.7 | async-start | bytes 1048576 | tf_op jit(solution)/shard_map/all_to_all | solution.py:12
  165.9 31.8 %copy-start.2 = (f32[64]{0:T(128)S(1)}, f32[64]{0:T(128)}, u32[]{:S(2)}) copy-start(f32[64]{0:T(128)} %param.26) | copy-start | bytes 772
  180.4 16.7 %all-to-all-start.8 = ((f32[32,40,128]{2,1,0:T(8,128)}), f32[32,40,128]{2,1,0:T(8,128)S(1)}, u32[]{:S(2)}, u32[]{:S(2)}) async-start(f32[32,40,128]{2,1,0:T(8,128)} %pad_maximum_fusion.3), calls=%async_computation.8 | async-start | bytes 1310720 | tf_op jit(solution)/shard_map/all_to_all | solution.py:12
  199.7 7.3 %collective-permute-start.3 = (f32[32,1024]{1,0:T(8,128)S(1)}, f32[32,1024]{1,0:T(8,128)S(1)}, u32[]{:S(2)}, u32[]{:S(2)}) collective-permute-start(f32[32,1024]{1,0:T(8,128)S(1)} %get-tuple-element.126), channel_id=1, source_target_pairs={{0,32},{32,64},{64,96},{96,0},{1,33},{33,65},{65,97},{97,1},{2,34}... | collective-permute-start | bytes 393224 | tf_op jit(solution)/shard_map/ppermute | solution.py:101
  208.4 15.0 %all-to-all-start.9 = ((f32[32,32,128]{2,1,0:T(8,128)}), f32[32,32,128]{2,1,0:T(8,128)S(1)}, u32[]{:S(2)}, u32[]{:S(2)}) async-start(f32[32,32,128]{2,1,0:T(8,128)} %gather_fusion.25), calls=%async_computation.9 | async-start | bytes 1048576 | tf_op jit(solution)/shard_map/all_to_all | solution.py:12
  227.5 16.6 %all-to-all-start.10 = ((f32[32,40,128]{2,1,0:T(8,128)}), f32[32,40,128]{2,1,0:T(8,128)S(1)}, u32[]{:S(2)}, u32[]{:S(2)}) async-start(f32[32,40,128]{2,1,0:T(8,128)} %pad_maximum_fusion.4), calls=%async_computation.10 | async-start | bytes 1310720 | tf_op jit(solution)/shard_map/all_to_all | solution.py:12
  231.7 15.9 %collective-permute-start.6 = (f32[16,1024]{1,0:T(8,128)S(1)}, f32[16,1024]{1,0:T(8,128)S(1)}, u32[]{:S(2)}, u32[]{:S(2)}) collective-permute-start(f32[16,1024]{1,0:T(8,128)S(1)} %get-tuple-element.139), channel_id=1, source_target_pairs={{96,0},{97,1},{98,2},{99,3},{100,4},{101,5},{102,6},{103,7},{104,8... | collective-permute-start | bytes 196616 | tf_op jit(solution)/shard_map/ppermute | solution.py:98
  233.0 14.6 %collective-permute-start.5 = (f32[16,1024]{1,0:T(8,128)S(1)}, f32[16,1024]{1,0:T(8,128)S(1)}, u32[]{:S(2)}, u32[]{:S(2)}) collective-permute-start(f32[16,1024]{1,0:T(8,128)S(1)} %get-tuple-element.140), channel_id=1, source_target_pairs={{96,32},{97,33},{98,34},{99,35},{100,36},{101,37},{102,38},{103,39... | collective-permute-start | bytes 196616 | tf_op jit(solution)/shard_map/ppermute | solution.py:98
  246.9 0.7 collective-permute-start.4

commit v4 on v3

--- a/solution.py
+++ b/solution.py
@@ -45,10 +45,10 @@
     from_e = want[:, last_m][:, None] == jnp.arange(blk_count, dtype=jnp.int32)[None, :]
     base_c = retain[last_m].reshape(blk_count, blk_size) + c_loc
 
-    def apply_month(state, j, c_all):
+    def apply_month(state, j, c_all, extra):
         sb = state.reshape(batch, blk_count, blk_size)
         out = jnp.take(sb, send_idx[:, j], axis=1, mode="clip").transpose(1, 0, 2)
-        if j == last_m:
+        if j == last_m and extra:
             part = jnp.sum(state * c_all[None, :], axis=1)
             row = jnp.zeros((devices, 8, blk_size), jnp.float32).at[:, 0, :batch].set(part[None, :])
             row = row.at[:, 1, :].set(cs_send)
@@ -87,7 +87,7 @@
         if step < NBATCH:
             held = jnp.where(section == 0, tracers[step * batch : (step + 1) * batch], held)
         for j in range(months_here):
-            held, inventory, c_all = apply_month(held, j, c_all)
+            held, inventory, c_all = apply_month(held, j, c_all, step == 0 or step >= sections - 1)
         b = step - last
         if b >= 0:
             scaled = held * (targets[b * batch : (b + 1) * batch] * points / inventory)[:, None]

time: 252 us -> 248 us (0.984)
    all_to_all x11, waiting for transfers between devices: 75.9 us -> 73.3 us  [exchange(): return lax.all_to_all(x, axis, 0, 0, tiled=True)]
where the time goes in v4:
time: 248 us; the launch traced here: 245 us
  waiting for transfers between devices  101 us (41%)
  starting transfers between devices  54.2 us (22%)
  matrix products  53.6 us (22%)
  local copies, waits for them, and re-layouts  26 us (10%)
  other arithmetic  9.41 us (4%)
    all_to_all x11, waiting for transfers between devices, exchange(): return lax.all_to_all(x, axis, 0, 0, tiled=True)  73.3 us
    all_to_all x11, starting transfers between devices, exchange(): return lax.all_to_all(x, axis, 0, 0, tiled=True)  49.3 us
    dot_general x10, matrix products, apply_month(): jnp.einsum('tbkc,bkrc->tbr', loc, blocks[j, :, :near], precision=PRECISIO...  35.1 us
    ppermute x4, waiting for transfers between devices, local(): lax.ppermute(held, 'month', [(i, (i + 1) % sections) for i in range(secti...  27.5 us
    dot_general x10, matrix products, apply_month(): jnp.einsum('tbkc,bkrc->tbr', far, blocks[j, :, near:], precision=PRECISIO...  18.5 us
    gather x10, local copies, waits for them, and re-layouts, apply_month(): out = jnp.take(sb, send_idx[:, j], axis=1, mode='clip').transpose(1, 0, 2)  11.4 us
    gather x10, local copies, waits for them, and re-layouts, apply_month(): jnp.take(sb, src_blk[j, :, :near].reshape(-1), axis=1, mode='clip')  6.09 us
    gather x10, local copies, waits for them, and re-layouts, apply_month(): jnp.take(got, src_dev[j, :, near:].reshape(-1), axis=1, mode='clip')  5.66 us
  transfers between devices with their start and end apart: 18, of which 15 were waited for; matrix products, arithmetic and copies ran while one was open for 20% of the time, Pallas kernels for 0%

profile of v4, /device:TPU:0, one launch (start us, length us, event | category | flops | bytes accessed | tf_op | source)
XLA Modules:
  0.0 244.9 jit_solution(14235331099726958495)
XLA Ops:
  0.0 0.8 add_select_fusion
  1.2 0.7 copy.99
  1.9 8.4 %all-to-all-start = ((s32[32,1,2]{2,1,0:T(1,128)}), s32[32,1,2]{2,1,0:T(1,128)S(1)}, u32[]{:S(2)}, u32[]{:S(2)}) async-start(s32[32,1,2]{2,1,0:T(1,128)} %copy.99), calls=%async_computation | async-start | bytes 32768 | tf_op jit(solution)/shard_map/all_to_all | solution.py:12
  10.9 2.6 %slice_reduce_fusion = f32[8,8,128]{2,1,0:T(8,128)S(1)} fusion(f32[2,8,8,128,128]{4,3,2,1,0:T(8,128)} %param.20), kind=kLoop, calls=%fused_computation.30 | loop fusion | flops 1040384 | bytes 4227072 | tf_op jit(solution)/shard_map/reduce_sum | solution.py:38
  13.8 0.9 copy_bitcast_fusion.9
  14.8 2.9 %all-to-all-done = s32[32,1,2]{2,1,0:T(1,128)S(1)} async-done(((s32[32,1,2]{2,1,0:T(1,128)}), s32[32,1,2]{2,1,0:T(1,128)S(1)}, u32[]{:S(2)}, u32[]{:S(2)}) %all-to-all-start) | async-done | bytes 288 | tf_op jit(solution)/shard_map/all_to_all | solution.py:12
  17.7 1.4 gather_fusion.1
  19.1 4.5 %all-to-all-start.1 = ((f32[32,32,128]{2,1,0:T(8,128)}), f32[32,32,128]{2,1,0:T(8,128)S(1)}, u32[]{:S(2)}, u32[]{:S(2)}) async-start(f32[32,32,128]{2,1,0:T(8,128)} %gather_fusion.1), calls=%async_computation.1 | async-start | bytes 1048576 | tf_op jit(solution)/shard_map/all_to_all | solution.py:12
  23.7 0.7 slice.284
  25.1 3.5 %fusion.50 = f32[8,32,128]{2,1,0:T(8,128)S(1)} fusion(f32[32,8,6,128]{3,0,2,1:T(8,128)S(1)} %bitcast.399, f32[2,8,8,128,128]{4,3,2,1,0:T(8,128)} %param.20), kind=kOutput, calls=%fused_computation.91 | convolution fusion | flops 150994944 | bytes 4063232 | tf_op jit(solution)/shard_map/tbkc,bkrc->tbr/dot_general | solution.py:66
  28.6 6.1 %all-to-all-done.1 = f32[32,32,128]{2,1,0:T(8,128)S(1)} async-done(((f32[32,32,128]{2,1,0:T(8,128)}), f32[32,32,128]{2,1,0:T(8,128)S(1)}, u32[]{:S(2)}, u32[]{:S(2)}) %all-to-all-start.1) | async-done | bytes 524320 | tf_op jit(solution)/shard_map/all_to_all | solution.py:12
  35.3 1.9 fusion.40
  38.0 0.9 pad_maximum_fusion
  38.9 4.1 %all-to-all-start.2 = ((f32[32,40,128]{2,1,0:T(8,128)}), f32[32,40,128]{2,1,0:T(8,128)S(1)}, u32[]{:S(2)}, u32[]{:S(2)}) async-start(f32[32,40,128]{2,1,0:T(8,128)} %pad_maximum_fusion), calls=%async_computation.2 | async-start | bytes 1310720 | tf_op jit(solution)/shard_map/all_to_all | solution.py:12
  43.8 3.5 %fusion.65 = f32[8,32,128]{2,1,0:T(8,128)S(1)} fusion(f32[32,8,6,128]{3,0,2,1:T(8,128)S(1)} %bitcast.402, f32[2,8,8,128,128]{4,3,2,1,0:T(8,128)} %param.20), kind=kOutput, calls=%fused_computation.96 | convolution fusion | flops 150994944 | bytes 4063232 | tf_op jit(solution)/shard_map/tbkc,bkrc->tbr/dot_general | solution.py:66
  47.3 8.3 %all-to-all-done.2 = f32[32,40,128]{2,1,0:T(8,128)S(1)} async-done(((f32[32,40,128]{2,1,0:T(8,128)}), f32[32,40,128]{2,1,0:T(8,128)S(1)}, u32[]{:S(2)}, u32[]{:S(2)}) %all-to-all-start.2) | async-done | bytes 655392 | tf_op jit(solution)/shard_map/all_to_all | solution.py:12
  56.4 1.9 fusion.41
  58.3 1.6 collective-permute-start
  59.8 5.8 %collective-permute-done = f32[32,1024]{1,0:T(8,128)S(1)} collective-permute-done((f32[32,1024]{1,0:T(8,128)S(1)}, f32[32,1024]{1,0:T(8,128)S(1)}, u32[]{:S(2)}, u32[]{:S(2)}) %collective-permute-start) | collective-permute-done | bytes 131104 | tf_op jit(solution)/shard_map/ppermute | solution.py:101
  65.6 1.4 gather_fusion.7
  67.0 3.9 %all-to-all-start.3 = ((f32[32,32,128]{2,1,0:T(8,128)}), f32[32,32,128]{2,1,0:T(8,128)S(1)}, u32[]{:S(2)}, u32[]{:S(2)}) async-start(f32[32,32,128]{2,1,0:T(8,128)} %gather_fusion.7), calls=%async_computation.3 | async-start | bytes 1048576 | tf_op jit(solution)/shard_map/all_to_all | solution.py:12
  71.5 3.5 %fusion.53 = f32[8,32,128]{2,1,0:T(8,128)S(1)} fusion(f32[32,8,6,128]{3,0,2,1:T(8,128)S(1)} %bitcast.403, f32[2,8,8,128,128]{4,3,2,1,0:T(8,128)} %param.20), kind=kOutput, calls=%fused_computation.92 | convolution fusion | flops 150994944 | bytes 4063232 | tf_op jit(solution)/shard_map/tbkc,bkrc->tbr/dot_general | solution.py:66
  75.0 6.9 %all-to-all-done.3 = f32[32,32,128]{2,1,0:T(8,128)S(1)} async-done(((f32[32,32,128]{2,1,0:T(8,128)}), f32[32,32,128]{2,1,0:T(8,128)S(1)}, u32[]{:S(2)}, u32[]{:S(2)}) %all-to-all-start.3) | async-done | bytes 524320 | tf_op jit(solution)/shard_map/all_to_all | solution.py:12
  82.6 1.9 fusion.42
  84.5 1.4 gather_fusion.10
  85.9 4.1 %all-to-all-start.4 = ((f32[32,32,128]{2,1,0:T(8,128)}), f32[32,32,128]{2,1,0:T(8,128)S(1)}, u32[]{:S(2)}, u32[]{:S(2)}) async-start(f32[32,32,128]{2,1,0:T(8,128)} %gather_fusion.10), calls=%async_computation.4 | async-start | bytes 1048576 | tf_op jit(solution)/shard_map/all_to_all | solution.py:12
  90.6 3.5 %fusion.68 = f32[8,32,128]{2,1,0:T(8,128)S(1)} fusion(f32[32,8,6,128]{3,0,2,1:T(8,128)S(1)} %bitcast.404, f32[2,8,8,128,128]{4,3,2,1,0:T(8,128)} %param.20), kind=kOutput, calls=%fused_computation.97 | convolution fusion | flops 150994944 | bytes 4063232 | tf_op jit(solution)/shard_map/tbkc,bkrc->tbr/dot_general | solution.py:66
  94.1 6.9 %all-to-all-done.4 = f32[32,32,128]{2,1,0:T(8,128)S(1)} async-done(((f32[32,32,128]{2,1,0:T(8,128)}), f32[32,32,128]{2,1,0:T(8,128)S(1)}, u32[]{:S(2)}, u32[]{:S(2)}) %all-to-all-start.4) | async-done | bytes 524320 | tf_op jit(solution)/shard_map/all_to_all | solution.py:12
  101.6 1.9 fusion.43
  104.0 7.1 %collective-permute-done.1 = f32[32,1024]{1,0:T(8,128)S(1)} collective-permute-done((f32[32,1024]{1,0:T(8,128)S(1)}, f32[32,1024]{1,0:T(8,128)S(1)}, u32[]{:S(2)}, u32[]{:S(2)}) %collective-permute-start.1) | collective-permute-done | bytes 131104 | tf_op jit(solution)/shard_map/ppermute | solution.py:101
  111.2 1.4 gather_fusion.13
  112.6 3.9 %all-to-all-start.5 = ((f32[32,32,128]{2,1,0:T(8,128)}), f32[32,32,128]{2,1,0:T(8,128)S(1)}, u32[]{:S(2)}, u32[]{:S(2)}) async-start(f32[32,32,128]{2,1,0:T(8,128)} %gather_fusion.13), calls=%async_computation.5 | async-start | bytes 1048576 | tf_op jit(solution)/shard_map/all_to_all | solution.py:12
  117.1 3.5 %fusion.56 = f32[8,32,128]{2,1,0:T(8,128)S(1)} fusion(f32[32,8,6,128]{3,0,2,1:T(8,128)S(1)} %bitcast.405, f32[2,8,8,128,128]{4,3,2,1,0:T(8,128)} %param.20), kind=kOutput, calls=%fused_computation.93 | convolution fusion | flops 150994944 | bytes 4063232 | tf_op jit(solution)/shard_map/tbkc,bkrc->tbr/dot_general | solution.py:66
  120.6 6.9 %all-to-all-done.5 = f32[32,32,128]{2,1,0:T(8,128)S(1)} async-done(((f32[32,32,128]{2,1,0:T(8,128)}), f32[32,32,128]{2,1,0:T(8,128)S(1)}, u32[]{:S(2)}, u32[]{:S(2)}) %all-to-all-start.5) | async-done | bytes 524320 | tf_op jit(solution)/shard_map/all_to_all | solution.py:12
  128.1 1.9 fusion.44
  130.0 1.4 gather_fusion.16
  131.4 4.1 %all-to-all-start.6 = ((f32[32,32,128]{2,1,0:T(8,128)}), f32[32,32,128]{2,1,0:T(8,128)S(1)}, u32[]{:S(2)}, u32[]{:S(2)}) async-start(f32[32,32,128]{2,1,0:T(8,128)} %gather_fusion.16), calls=%async_computation.6 | async-start | bytes 1048576 | tf_op jit(solution)/shard_map/all_to_all | solution.py:12
  136.1 3.5 %fusion.71 = f32[8,32,128]{2,1,0:T(8,128)S(1)} fusion(f32[32,8,6,128]{3,0,2,1:T(8,128)S(1)} %bitcast.406, f32[2,8,8,128,128]{4,3,2,1,0:T(8,128)} %param.20), kind=kOutput, calls=%fused_computation.98 | convolution fusion | flops 150994944 | bytes 4063232 | tf_op jit(solution)/shard_map/tbkc,bkrc->tbr/dot_general | solution.py:66
  139.6 6.9 %all-to-all-done.6 = f32[32,32,128]{2,1,0:T(8,128)S(1)} async-done(((f32[32,32,128]{2,1,0:T(8,128)}), f32[32,32,128]{2,1,0:T(8,128)S(1)}, u32[]{:S(2)}, u32[]{:S(2)}) %all-to-all-start.6) | async-done | bytes 524320 | tf_op jit(solution)/shard_map/all_to_all | solution.py:12
  147.1 1.9 fusion.45
  149.1 7.4 %collective-permute-done.2 = f32[32,1024]{1,0:T(8,128)S(1)} collective-permute-done((f32[32,1024]{1,0:T(8,128)S(1)}, f32[32,1024]{1,0:T(8,128)S(1)}, u32[]{:S(2)}, u32[]{:S(2)}) %collective-permute-start.2) | collective-permute-done | bytes 131104 | tf_op jit(solution)/shard_map/ppermute | solution.py:101
  156.5 1.4 gather_fusion.19
  157.9 3.9 %all-to-all-start.7 = ((f32[32,32,128]{2,1,0:T(8,128)}), f32[32,32,128]{2,1,0:T(8,128)S(1)}, u32[]{:S(2)}, u32[]{:S(2)}) async-start(f32[32,32,128]{2,1,0:T(8,128)} %gather_fusion.19), calls=%async_computation.7 | async-start | bytes 1048576 | tf_op jit(solution)/shard_map/all_to_all | solution.py:12
  162.4 3.5 %fusion.59 = f32[8,32,128]{2,1,0:T(8,128)S(1)} fusion(f32[32,8,6,128]{3,0,2,1:T(8,128)S(1)} %bitcast.407, f32[2,8,8,128,128]{4,3,2,1,0:T(8,128)} %param.20), kind=kOutput, calls=%fused_computation.94 | convolution fusion | flops 150994944 | bytes 4063232 | tf_op jit(solution)/shard_map/tbkc,bkrc->tbr/dot_general | solution.py:66
  165.9 6.9 %all-to-all-done.7 = f32[32,32,128]{2,1,0:T(8,128)S(1)} async-done(((f32[32,32,128]{2,1,0:T(8,128)}), f32[32,32,128]{2,1,0:T(8,128)S(1)}, u32[]{:S(2)}, u32[]{:S(2)}) %all-to-all-start.7) | async-done | bytes 524320 | tf_op jit(solution)/shard_map/all_to_all | solution.py:12
  173.4 1.9 fusion.46
  176.2 0.9 pad_maximum_fusion.1
  177.0 4.1 %all-to-all-start.8 = ((f32[32,40,128]{2,1,0:T(8,128)}), f32[32,40,128]{2,1,0:T(8,128)S(1)}, u32[]{:S(2)}, u32[]{:S(2)}) async-start(f32[32,40,128]{2,1,0:T(8,128)} %pad_maximum_fusion.1), calls=%async_computation.8 | async-start | bytes 1310720 | tf_op jit(solution)/shard_map/all_to_all | solution.py:12
  181.8 3.5 %fusion.74 = f32[8,32,128]{2,1,0:T(8,128)S(1)} fusion(f32[32,8,6,128]{3,0,2,1:T(8,128)S(1)} %bitcast.408, f32[2,8,8,128,128]{4,3,2,1,0:T(8,128)} %param.20), kind=kOutput, calls=%fused_computation.99 | convolution fusion | flops 150994944 | bytes 4063232 | tf_op jit(solution)/shard_map/tbkc,bkrc->tbr/dot_general | solution.py:66
  185.3 8.4 %all-to-all-done.8 = f32[32,40,128]{2,1,0:T(8,128)S(1)} async-done(((f32[32,40,128]{2,1,0:T(8,128)}), f32[32,40,128]{2,1,0:T(8,128)S(1)}, u32[]{:S(2)}, u32[]{:S(2)}) %all-to-all-start.8) | async-done | bytes 655392 | tf_op jit(solution)/shard_map/all_to_all | solution.py:12
  194.4 1.9 fusion.47
  196.5 7.2 %collective-permute-done.3 = f32[32,1024]{1,0:T(8,128)S(1)} collective-permute-done((f32[32,1024]{1,0:T(8,128)S(1)}, f32[32,1024]{1,0:T(8,128)S(1)}, u32[]{:S(2)}, u32[]{:S(2)}) %collective-permute-start.3) | collective-permute-done | bytes 131104 | tf_op jit(solution)/shard_map/ppermute | solution.py:101
  203.7 1.4 gather_fusion.25
  205.1 4.1 %all-to-all-start.9 = ((f32[32,32,128]{2,1,0:T(8,128)}), f32[32,32,128]{2,1,0:T(8,128)S(1)}, u32[]{:S(2)}, u32[]{:S(2)}) async-start(f32[32,32,128]{2,1,0:T(8,128)} %gather_fusion.25), calls=%async_computation.9 | async-start | bytes 1048576 | tf_op jit(solution)/shard_map/all_to_all | solution.py:12
  209.9 3.5 %fusion.62 = f32[8,32,128]{2,1,0:T(8,128)S(1)} fusion(f32[32,8,6,128]{3,0,2,1:T(8,128)S(1)} %bitcast.400, f32[2,8,8,128,128]{4,3,2,1,0:T(8,128)} %param.20), kind=kOutput, calls=%fused_computation.95 | convolution fusion | flops 150994944 | bytes 4063232 | tf_op jit(solution)/shard_map/tbkc,bkrc->tbr/dot_general | solution.py:66
  213.5 6.6 %all-to-all-done.9 = f32[32,32,128]{2,1,0:T(8,128)S(1)} async-done(((f32[32,32,128]{2,1,0:T(8,128)}), f32[32,32,128]{2,1,0:T(8,128)S(1)}, u32[]{:S(2)}, u32[]{:S(2)}) %all-to-all-start.9) | async-done | bytes 524320 | tf_op jit(solution)/shard_map/all_to_all | solution.py:12
  220.6 1.9 fusion.48
  223.3 0.9 pad_maximum_fusion.2
  224.2 4.1 %all-to-all-start.10 = ((f32[32,40,128]{2,1,0:T(8,128)}), f32[32,40,128]{2,1,0:T(8,128)S(1)}, u32[]{:S(2)}, u32[]{:S(2)}) async-start(f32[32,40,128]{2,1,0:T(8,128)} %pad_maximum_fusion.2), calls=%async_computation.10 | async-start | bytes 1310720 | tf_op jit(solution)/shard_map/all_to_all | solution.py:12
  228.4 1.3 collective-permute-start.6
  229.7 0.7 collective-permute-start.5
  230.9 3.5 %fusion.77 = f32[8,32,128]{2,1,0:T(8,128)S(1)} fusion(f32[32,8,6,128]{3,0,2,1:T(8,128)S(1)} %bitcast.401, f32[2,8,8,128,128]{4,3,2,1,0:T(8,128)} %param.20), kind=kOutput, calls=%fused_computation.100 | convolution fusion | flops 150994944 | bytes 4063232 | tf_op jit(solution)/shard_map/tbkc,bkrc->tbr/dot_general | solution.py:66
  234.5 6.4 %all-to-all-done.10 = f32[32,40,128]{2,1,0:T(8,128)S(1)} async-done(((f32[32,40,128]{2,1,0:T(8,128)}), f32[32,40,128]{2,1,0:T(8,128)S(1)}, u32[]{:S(2)}, u32[]{:S(2)}) %all-to-all-start.10) | async-done | bytes 655392 | tf_op jit(solution)/shard_map/all_to_all | solution.py:12
  241.6 1.8 fusion.49
  (109 shorter events, 18.7 us)
Async XLA Ops:
  0.0 37.2 %copy-start = (f32[64,1024]{1,0:T(8,128)S(1)}, f32[64,1024]{1,0:T(8,128)}, u32[]{:S(2)}) copy-start(f32[64,1024]{1,0:T(8,128)} %param.17) | copy-start | bytes 786436
  1.9 15.8 %all-to-all-start = ((s32[32,1,2]{2,1,0:T(1,128)}), s32[32,1,2]{2,1,0:T(1,128)S(1)}, u32[]{:S(2)}, u32[]{:S(2)}) async-start(s32[32,1,2]{2,1,0:T(1,128)} %copy.99), calls=%async_computation | async-start | bytes 32768 | tf_op jit(solution)/shard_map/all_to_all | solution.py:12
  19.1 15.6 %all-to-all-start.1 = ((f32[32,32,128]{2,1,0:T(8,128)}), f32[32,32,128]{2,1,0:T(8,128)S(1)}, u32[]{:S(2)}, u32[]{:S(2)}) async-start(f32[32,32,128]{2,1,0:T(8,128)} %gather_fusion.1), calls=%async_computation.1 | async-start | bytes 1048576 | tf_op jit(solution)/shard_map/all_to_all | solution.py:12
  25.1 31.3 %copy-start.1 = (f32[2,1024]{1,0:T(2,128)S(1)}, f32[2,1024]{1,0:T(2,128)}, u32[]{:S(2)}) copy-start(f32[2,1024]{1,0:T(2,128)} %param.19) | copy-start | bytes 24580
  38.9 16.7 %all-to-all-start.2 = ((f32[32,40,128]{2,1,0:T(8,128)}), f32[32,40,128]{2,1,0:T(8,128)S(1)}, u32[]{:S(2)}, u32[]{:S(2)}) async-start(f32[32,40,128]{2,1,0:T(8,128)} %pad_maximum_fusion), calls=%async_computation.2 | async-start | bytes 1310720 | tf_op jit(solution)/shard_map/all_to_all | solution.py:12
  58.3 7.3 %collective-permute-start = (f32[32,1024]{1,0:T(8,128)S(1)}, f32[32,1024]{1,0:T(8,128)S(1)}, u32[]{:S(2)}, u32[]{:S(2)}) collective-permute-start(f32[32,1024]{1,0:T(8,128)S(1)} %bitcast_add_fusion.8), channel_id=1, source_target_pairs={{0,32},{32,64},{64,96},{96,0},{1,33},{33,65},{65,97},{97,1},{2,34}... | collective-permute-start | bytes 393224 | tf_op jit(solution)/shard_map/ppermute | solution.py:101
  67.0 15.0 %all-to-all-start.3 = ((f32[32,32,128]{2,1,0:T(8,128)}), f32[32,32,128]{2,1,0:T(8,128)S(1)}, u32[]{:S(2)}, u32[]{:S(2)}) async-start(f32[32,32,128]{2,1,0:T(8,128)} %gather_fusion.7), calls=%async_computation.3 | async-start | bytes 1048576 | tf_op jit(solution)/shard_map/all_to_all | solution.py:12
  85.9 15.2 %all-to-all-start.4 = ((f32[32,32,128]{2,1,0:T(8,128)}), f32[32,32,128]{2,1,0:T(8,128)S(1)}, u32[]{:S(2)}, u32[]{:S(2)}) async-start(f32[32,32,128]{2,1,0:T(8,128)} %gather_fusion.10), calls=%async_computation.4 | async-start | bytes 1048576 | tf_op jit(solution)/shard_map/all_to_all | solution.py:12
  103.5 7.7 %collective-permute-start.1 = (f32[32,1024]{1,0:T(8,128)S(1)}, f32[32,1024]{1,0:T(8,128)S(1)}, u32[]{:S(2)}, u32[]{:S(2)}) collective-permute-start(f32[32,1024]{1,0:T(8,128)S(1)} %bitcast_add_fusion.6), channel_id=1, source_target_pairs={{0,32},{32,64},{64,96},{96,0},{1,33},{33,65},{65,97},{97,1},{2,34}... | collective-permute-start | bytes 393224 | tf_op jit(solution)/shard_map/ppermute | solution.py:101
  112.6 15.0 %all-to-all-start.5 = ((f32[32,32,128]{2,1,0:T(8,128)}), f32[32,32,128]{2,1,0:T(8,128)S(1)}, u32[]{:S(2)}, u32[]{:S(2)}) async-start(f32[32,32,128]{2,1,0:T(8,128)} %gather_fusion.13), calls=%async_computation.5 | async-start | bytes 1048576 | tf_op jit(solution)/shard_map/all_to_all | solution.py:12
  131.4 15.2 %all-to-all-start.6 = ((f32[32,32,128]{2,1,0:T(8,128)}), f32[32,32,128]{2,1,0:T(8,128)S(1)}, u32[]{:S(2)}, u32[]{:S(2)}) async-start(f32[32,32,128]{2,1,0:T(8,128)} %gather_fusion.16), calls=%async_computation.6 | async-start | bytes 1048576 | tf_op jit(solution)/shard_map/all_to_all | solution.py:12
  149.0 7.5 %collective-permute-start.2 = (f32[32,1024]{1,0:T(8,128)S(1)}, f32[32,1024]{1,0:T(8,128)S(1)}, u32[]{:S(2)}, u32[]{:S(2)}) collective-permute-start(f32[32,1024]{1,0:T(8,128)S(1)} %bitcast_add_fusion.4), channel_id=1, source_target_pairs={{0,32},{32,64},{64,96},{96,0},{1,33},{33,65},{65,97},{97,1},{2,34}... | collective-permute-start | bytes 393224 | tf_op jit(solution)/shard_map/ppermute | solution.py:101
  157.9 15.0 %all-to-all-start.7 = ((f32[32,32,128]{2,1,0:T(8,128)}), f32[32,32,128]{2,1,0:T(8,128)S(1)}, u32[]{:S(2)}, u32[]{:S(2)}) async-start(f32[32,32,128]{2,1,0:T(8,128)} %gather_fusion.19), calls=%async_computation.7 | async-start | bytes 1048576 | tf_op jit(solution)/shard_map/all_to_all | solution.py:12
  162.4 32.0 %copy-start.2 = (f32[64]{0:T(128)S(1)}, f32[64]{0:T(128)}, u32[]{:S(2)}) copy-start(f32[64]{0:T(128)} %param.18) | copy-start | bytes 772
  177.0 16.7 %all-to-all-start.8 = ((f32[32,40,128]{2,1,0:T(8,128)}), f32[32,40,128]{2,1,0:T(8,128)S(1)}, u32[]{:S(2)}, u32[]{:S(2)}) async-start(f32[32,40,128]{2,1,0:T(8,128)} %pad_maximum_fusion.1), calls=%async_computation.8 | async-start | bytes 1310720 | tf_op jit(solution)/shard_map/all_to_all | solution.py:12
  196.3 7.3 %collective-permute-start.3 = (f32[32,1024]{1,0:T(8,128)S(1)}, f32[32,1024]{1,0:T(8,128)S(1)}, u32[]{:S(2)}, u32[]{:S(2)}) collective-permute-start(f32[32,1024]{1,0:T(8,128)S(1)} %get-tuple-element.78), channel_id=1, source_target_pairs={{0,32},{32,64},{64,96},{96,0},{1,33},{33,65},{65,97},{97,1},{2,34}... | collective-permute-start | bytes 393224 | tf_op jit(solution)/shard_map/ppermute | solution.py:101
  205.1 15.0 %all-to-all-start.9 = ((f32[32,32,128]{2,1,0:T(8,128)}), f32[32,32,128]{2,1,0:T(8,128)S(1)}, u32[]{:S(2)}, u32[]{:S(2)}) async-start(f32[32,32,128]{2,1,0:T(8,128)} %gather_fusion.25), calls=%async_computation.9 | async-start | bytes 1048576 | tf_op jit(solution)/shard_map/all_to_all | solution.py:12
  224.2 16.7 %all-to-all-start.10 = ((f32[32,40,128]{2,1,0:T(8,128)}), f32[32,40,128]{2,1,0:T(8,128)S(1)}, u32[]{:S(2)}, u32[]{:S(2)}) async-start(f32[32,40,128]{2,1,0:T(8,128)} %pad_maximum_fusion.2), calls=%async_computation.10 | async-start | bytes 1310720 | tf_op jit(solution)/shard_map/all_to_all | solution.py:12
  228.4 15.9 %collective-permute-start.6 = (f32[16,1024]{1,0:T(8,128)S(1)}, f32[16,1024]{1,0:T(8,128)S(1)}, u32[]{:S(2)}, u32[]{:S(2)}) collective-permute-start(f32[16,1024]{1,0:T(8,128)S(1)} %get-tuple-element.85), channel_id=1, source_target_pairs={{96,0},{97,1},{98,2},{99,3},{100,4},{101,5},{102,6},{103,7},{104,8... | collective-permute-start | bytes 196616 | tf_op jit(solution)/shard_map/ppermute | solution.py:98
  229.7 14.6 %collective-permute-start.5 = (f32[16,1024]{1,0:T(8,128)S(1)}, f32[16,1024]{1,0:T(8,128)S(1)}, u32[]{:S(2)}, u32[]{:S(2)}) collective-permute-start(f32[16,1024]{1,0:T(8,128)S(1)} %get-tuple-element.86), channel_id=1, source_target_pairs={{96,32},{97,33},{98,34},{99,35},{100,36},{101,37},{102,38},{103,39... | collective-permute-start | bytes 196616 | tf_op jit(solution)/shard_map/ppermute | solution.py:98
  243.6 0.7 collective-permute-start.4

commit v5 on v4

--- a/solution.py
+++ b/solution.py
@@ -35,28 +35,27 @@
     req = jnp.sum(jnp.where(hit, far_blk[:, None, :] + 1, 0), axis=2) - 1
 
     last_m = months_here - 1
-    colsum = jnp.sum(blocks[last_m], axis=2)
+    colsum = jnp.sum(blocks[last_m, :, :near], axis=2)
     to_blk = src_blk[last_m, :, :near][:, :, None] == jnp.arange(blk_count, dtype=jnp.int32)[None, None, :]
-    c_loc = jnp.sum(jnp.where(to_blk[:, :, :, None], colsum[:, :near, None, :], 0.0), axis=(0, 1))
-    far_cs = colsum[:, near:].reshape(-1, blk_size)
+    c_loc = jnp.sum(jnp.where(to_blk[:, :, :, None], colsum[:, :, None, :], 0.0), axis=(0, 1))
+    far_cs = jnp.sum(blocks[last_m, :, near:], axis=2).reshape(-1, blk_size)
     cs_send = jnp.sum(jnp.where(hit[last_m][:, :, None], far_cs[None], 0.0), axis=1)
-    want = exchange(req.T, "grid")
+    recv = exchange(jnp.concatenate([cs_send, req.T.astype(jnp.float32)], axis=1), "grid")
+    want = jnp.round(recv[:, blk_size:]).astype(jnp.int32)
     send_idx = jnp.maximum(want, 0)
     from_e = want[:, last_m][:, None] == jnp.arange(blk_count, dtype=jnp.int32)[None, :]
-    base_c = retain[last_m].reshape(blk_count, blk_size) + c_loc
+    c_far = jnp.sum(jnp.where(from_e[:, :, None], recv[:, None, :blk_size], 0.0), axis=0)
+    c_all = (retain[last_m].reshape(blk_count, blk_size) + c_loc + c_far).reshape(rows_here)
 
-    def apply_month(state, j, c_all, extra):
+    def apply_month(state, j, extra):
         sb = state.reshape(batch, blk_count, blk_size)
         out = jnp.take(sb, send_idx[:, j], axis=1, mode="clip").transpose(1, 0, 2)
         if j == last_m and extra:
             part = jnp.sum(state * c_all[None, :], axis=1)
             row = jnp.zeros((devices, 8, blk_size), jnp.float32).at[:, 0, :batch].set(part[None, :])
-            row = row.at[:, 1, :].set(cs_send)
             full = exchange(jnp.concatenate([out, row], axis=1), "grid")
             inventory = jnp.sum(full[:, batch, :batch], axis=0)
             got = full[:, :batch].transpose(1, 0, 2)
-            c_far = jnp.sum(jnp.where(from_e[:, :, None], full[:, None, batch + 1, :], 0.0), axis=0)
-            c_all = (base_c + c_far).reshape(rows_here)
         else:
             inventory = None
             got = exchange(out, "grid")
@@ -76,10 +75,9 @@
             precision=PRECISION,
             preferred_element_type=jnp.float32,
         )
-        return retain[j][None, :] * state + mixed.reshape(batch, rows_here), inventory, c_all
+        return retain[j][None, :] * state + mixed.reshape(batch, rows_here), inventory
 
     held = jnp.zeros((batch, rows_here), jnp.float32)
-    c_all = jnp.zeros((rows_here,), jnp.float32)
     result = jnp.zeros((own, rows_here), jnp.float32)
     last = sections - 1
     steps = NBATCH + sections - 1
@@ -87,7 +85,7 @@
         if step < NBATCH:
             held = jnp.where(section == 0, tracers[step * batch : (step + 1) * batch], held)
         for j in range(months_here):
-            held, inventory, c_all = apply_month(held, j, c_all, step == 0 or step >= sections - 1)
+            held, inventory = apply_month(held, j, step >= sections - 1)
         b = step - last
         if b >= 0:
             scaled = held * (targets[b * batch : (b + 1) * batch] * points / inventory)[:, None]

time: 248 us -> 252 us (1.016)
  starting transfers between devices: 54.2 us -> 57 us
    all_to_all x11, starting transfers between devices: 49.3 us -> 52.4 us  [exchange(): return lax.all_to_all(x, axis, 0, 0, tiled=True)]
  transfers between devices with their start and end apart: 18 -> 18, of which waited for: 15 -> 14; matrix products, arithmetic and copies ran while one was open for 20% -> 19% of each run, Pallas kernels for 0% -> 0%
where the time goes in v5:
time: 252 us; the launch traced here: 248 us
  waiting for transfers between devices  101 us (40%)
  starting transfers between devices  57 us (23%)
  matrix products  53.6 us (21%)
  local copies, waits for them, and re-layouts  26 us (10%)
  other arithmetic  9.21 us (4%)
    all_to_all x11, waiting for transfers between devices, exchange(): return lax.all_to_all(x, axis, 0, 0, tiled=True)  73.8 us
    all_to_all x11, starting transfers between devices, exchange(): return lax.all_to_all(x, axis, 0, 0, tiled=True)  52.4 us
    dot_general x10, matrix products, apply_month(): jnp.einsum('tbkc,bkrc->tbr', loc, blocks[j, :, :near], precision=PRECISIO...  35.1 us
    ppermute x4, waiting for transfers between devices, local(): lax.ppermute(held, 'month', [(i, (i + 1) % sections) for i in range(secti...  27.7 us
    dot_general x10, matrix products, apply_month(): jnp.einsum('tbkc,bkrc->tbr', far, blocks[j, :, near:], precision=PRECISIO...  18.5 us
    gather x10, local copies, waits for them, and re-layouts, apply_month(): out = jnp.take(sb, send_idx[:, j], axis=1, mode='clip').transpose(1, 0, 2)  12.2 us
    gather x10, local copies, waits for them, and re-layouts, apply_month(): jnp.take(sb, src_blk[j, :, :near].reshape(-1), axis=1, mode='clip')  6.09 us
    gather x10, local copies, waits for them, and re-layouts, apply_month(): jnp.take(got, src_dev[j, :, near:].reshape(-1), axis=1, mode='clip')  5.66 us
  transfers between devices with their start and end apart: 18, of which 14 were waited for; matrix products, arithmetic and copies ran while one was open for 19% of the time, Pallas kernels for 0%

profile of v5, /device:TPU:0, one launch (start us, length us, event | category | flops | bytes accessed | tf_op | source)
XLA Modules:
  0.0 248.2 jit_solution(9029332305641759075)
XLA Ops:
  0.0 1.4 slice_reduce_fusion.1
  1.4 0.7 add_select_fusion
  3.6 8.4 %all-to-all-start = ((f32[32,1,130]{2,1,0:T(1,128)}), f32[32,1,130]{2,1,0:T(1,128)S(1)}, u32[]{:S(2)}, u32[]{:S(2)}) async-start(f32[32,1,130]{2,1,0:T(1,128)} %all_to_all.38), calls=%async_computation | async-start | bytes 65536 | tf_op jit(solution)/shard_map/all_to_all | solution.py:12
  12.1 2.2 slice_reduce_fusion
  14.6 0.9 copy_bitcast_fusion.9
  16.1 3.5 %fusion.50 = f32[8,32,128]{2,1,0:T(8,128)S(1)} fusion(f32[32,8,6,128]{3,0,2,1:T(8,128)S(1)} %bitcast.397, f32[2,8,8,128,128]{4,3,2,1,0:T(8,128)} %param.12), kind=kOutput, calls=%fused_computation.91 | convolution fusion | flops 150994944 | bytes 4063232 | tf_op jit(solution)/shard_map/tbkc,bkrc->tbr/dot_general | solution.py:65
  20.2 1.4 gather_fusion.1
  21.6 7.4 %all-to-all-start.1 = ((f32[32,32,128]{2,1,0:T(8,128)}), f32[32,32,128]{2,1,0:T(8,128)S(1)}, u32[]{:S(2)}, u32[]{:S(2)}) async-start(f32[32,32,128]{2,1,0:T(8,128)} %gather_fusion.1), calls=%async_computation.1 | async-start | bytes 1048576 | tf_op jit(solution)/shard_map/all_to_all | solution.py:12
  29.2 10.8 %all-to-all-done.1 = f32[32,32,128]{2,1,0:T(8,128)S(1)} async-done(((f32[32,32,128]{2,1,0:T(8,128)}), f32[32,32,128]{2,1,0:T(8,128)S(1)}, u32[]{:S(2)}, u32[]{:S(2)}) %all-to-all-start.1) | async-done | bytes 524320 | tf_op jit(solution)/shard_map/all_to_all | solution.py:12
  40.6 1.9 fusion.40
  42.5 1.4 gather_fusion.4
  43.9 4.1 %all-to-all-start.2 = ((f32[32,32,128]{2,1,0:T(8,128)}), f32[32,32,128]{2,1,0:T(8,128)S(1)}, u32[]{:S(2)}, u32[]{:S(2)}) async-start(f32[32,32,128]{2,1,0:T(8,128)} %gather_fusion.4), calls=%async_computation.2 | async-start | bytes 1048576 | tf_op jit(solution)/shard_map/all_to_all | solution.py:12
  48.8 3.5 %fusion.65 = f32[8,32,128]{2,1,0:T(8,128)S(1)} fusion(f32[32,8,6,128]{3,0,2,1:T(8,128)S(1)} %bitcast.390, f32[2,8,8,128,128]{4,3,2,1,0:T(8,128)} %param.12), kind=kOutput, calls=%fused_computation.96 | convolution fusion | flops 150994944 | bytes 4063232 | tf_op jit(solution)/shard_map/tbkc,bkrc->tbr/dot_general | solution.py:65
  52.3 6.8 %all-to-all-done.2 = f32[32,32,128]{2,1,0:T(8,128)S(1)} async-done(((f32[32,32,128]{2,1,0:T(8,128)}), f32[32,32,128]{2,1,0:T(8,128)S(1)}, u32[]{:S(2)}, u32[]{:S(2)}) %all-to-all-start.2) | async-done | bytes 524320 | tf_op jit(solution)/shard_map/all_to_all | solution.py:12
  59.7 1.9 fusion.41
  61.6 1.6 collective-permute-start
  63.1 5.9 %collective-permute-done = f32[32,1024]{1,0:T(8,128)S(1)} collective-permute-done((f32[32,1024]{1,0:T(8,128)S(1)}, f32[32,1024]{1,0:T(8,128)S(1)}, u32[]{:S(2)}, u32[]{:S(2)}) %collective-permute-start) | collective-permute-done | bytes 131104 | tf_op jit(solution)/shard_map/ppermute | solution.py:99
  69.1 1.4 gather_fusion.7
  70.4 3.9 %all-to-all-start.3 = ((f32[32,32,128]{2,1,0:T(8,128)}), f32[32,32,128]{2,1,0:T(8,128)S(1)}, u32[]{:S(2)}, u32[]{:S(2)}) async-start(f32[32,32,128]{2,1,0:T(8,128)} %gather_fusion.7), calls=%async_computation.3 | async-start | bytes 1048576 | tf_op jit(solution)/shard_map/all_to_all | solution.py:12
  75.0 3.5 %fusion.53 = f32[8,32,128]{2,1,0:T(8,128)S(1)} fusion(f32[32,8,6,128]{3,0,2,1:T(8,128)S(1)} %bitcast.391, f32[2,8,8,128,128]{4,3,2,1,0:T(8,128)} %param.12), kind=kOutput, calls=%fused_computation.92 | convolution fusion | flops 150994944 | bytes 4063232 | tf_op jit(solution)/shard_map/tbkc,bkrc->tbr/dot_general | solution.py:65
  78.5 6.9 %all-to-all-done.3 = f32[32,32,128]{2,1,0:T(8,128)S(1)} async-done(((f32[32,32,128]{2,1,0:T(8,128)}), f32[32,32,128]{2,1,0:T(8,128)S(1)}, u32[]{:S(2)}, u32[]{:S(2)}) %all-to-all-start.3) | async-done | bytes 524320 | tf_op jit(solution)/shard_map/all_to_all | solution.py:12
  86.0 1.9 fusion.42
  87.9 1.4 gather_fusion.10
  89.3 4.1 %all-to-all-start.4 = ((f32[32,32,128]{2,1,0:T(8,128)}), f32[32,32,128]{2,1,0:T(8,128)S(1)}, u32[]{:S(2)}, u32[]{:S(2)}) async-start(f32[32,32,128]{2,1,0:T(8,128)} %gather_fusion.10), calls=%async_computation.4 | async-start | bytes 1048576 | tf_op jit(solution)/shard_map/all_to_all | solution.py:12
  94.0 3.5 %fusion.68 = f32[8,32,128]{2,1,0:T(8,128)S(1)} fusion(f32[32,8,6,128]{3,0,2,1:T(8,128)S(1)} %bitcast.392, f32[2,8,8,128,128]{4,3,2,1,0:T(8,128)} %param.12), kind=kOutput, calls=%fused_computation.97 | convolution fusion | flops 150994944 | bytes 4063232 | tf_op jit(solution)/shard_map/tbkc,bkrc->tbr/dot_general | solution.py:65
  97.5 6.9 %all-to-all-done.4 = f32[32,32,128]{2,1,0:T(8,128)S(1)} async-done(((f32[32,32,128]{2,1,0:T(8,128)}), f32[32,32,128]{2,1,0:T(8,128)S(1)}, u32[]{:S(2)}, u32[]{:S(2)}) %all-to-all-start.4) | async-done | bytes 524320 | tf_op jit(solution)/shard_map/all_to_all | solution.py:12
  105.0 1.9 fusion.43
  107.3 7.1 %collective-permute-done.1 = f32[32,1024]{1,0:T(8,128)S(1)} collective-permute-done((f32[32,1024]{1,0:T(8,128)S(1)}, f32[32,1024]{1,0:T(8,128)S(1)}, u32[]{:S(2)}, u32[]{:S(2)}) %collective-permute-start.1) | collective-permute-done | bytes 131104 | tf_op jit(solution)/shard_map/ppermute | solution.py:99
  114.4 1.4 gather_fusion.13
  115.8 4.1 %all-to-all-start.5 = ((f32[32,32,128]{2,1,0:T(8,128)}), f32[32,32,128]{2,1,0:T(8,128)S(1)}, u32[]{:S(2)}, u32[]{:S(2)}) async-start(f32[32,32,128]{2,1,0:T(8,128)} %gather_fusion.13), calls=%async_computation.5 | async-start | bytes 1048576 | tf_op jit(solution)/shard_map/all_to_all | solution.py:12
  120.5 3.5 %fusion.56 = f32[8,32,128]{2,1,0:T(8,128)S(1)} fusion(f32[32,8,6,128]{3,0,2,1:T(8,128)S(1)} %bitcast.393, f32[2,8,8,128,128]{4,3,2,1,0:T(8,128)} %param.12), kind=kOutput, calls=%fused_computation.93 | convolution fusion | flops 150994944 | bytes 4063232 | tf_op jit(solution)/shard_map/tbkc,bkrc->tbr/dot_general | solution.py:65
  124.0 6.9 %all-to-all-done.5 = f32[32,32,128]{2,1,0:T(8,128)S(1)} async-done(((f32[32,32,128]{2,1,0:T(8,128)}), f32[32,32,128]{2,1,0:T(8,128)S(1)}, u32[]{:S(2)}, u32[]{:S(2)}) %all-to-all-start.5) | async-done | bytes 524320 | tf_op jit(solution)/shard_map/all_to_all | solution.py:12
  131.5 1.9 fusion.44
  133.4 1.4 gather_fusion.16
  134.8 4.1 %all-to-all-start.6 = ((f32[32,32,128]{2,1,0:T(8,128)}), f32[32,32,128]{2,1,0:T(8,128)S(1)}, u32[]{:S(2)}, u32[]{:S(2)}) async-start(f32[32,32,128]{2,1,0:T(8,128)} %gather_fusion.16), calls=%async_computation.6 | async-start | bytes 1048576 | tf_op jit(solution)/shard_map/all_to_all | solution.py:12
  139.5 3.5 %fusion.71 = f32[8,32,128]{2,1,0:T(8,128)S(1)} fusion(f32[32,8,6,128]{3,0,2,1:T(8,128)S(1)} %bitcast.394, f32[2,8,8,128,128]{4,3,2,1,0:T(8,128)} %param.12), kind=kOutput, calls=%fused_computation.98 | convolution fusion | flops 150994944 | bytes 4063232 | tf_op jit(solution)/shard_map/tbkc,bkrc->tbr/dot_general | solution.py:65
  143.0 6.9 %all-to-all-done.6 = f32[32,32,128]{2,1,0:T(8,128)S(1)} async-done(((f32[32,32,128]{2,1,0:T(8,128)}), f32[32,32,128]{2,1,0:T(8,128)S(1)}, u32[]{:S(2)}, u32[]{:S(2)}) %all-to-all-start.6) | async-done | bytes 524320 | tf_op jit(solution)/shard_map/all_to_all | solution.py:12
  150.5 1.9 fusion.45
  152.5 7.4 %collective-permute-done.2 = f32[32,1024]{1,0:T(8,128)S(1)} collective-permute-done((f32[32,1024]{1,0:T(8,128)S(1)}, f32[32,1024]{1,0:T(8,128)S(1)}, u32[]{:S(2)}, u32[]{:S(2)}) %collective-permute-start.2) | collective-permute-done | bytes 131104 | tf_op jit(solution)/shard_map/ppermute | solution.py:99
  159.9 1.4 gather_fusion.19
  161.3 3.9 %all-to-all-start.7 = ((f32[32,32,128]{2,1,0:T(8,128)}), f32[32,32,128]{2,1,0:T(8,128)S(1)}, u32[]{:S(2)}, u32[]{:S(2)}) async-start(f32[32,32,128]{2,1,0:T(8,128)} %gather_fusion.19), calls=%async_computation.7 | async-start | bytes 1048576 | tf_op jit(solution)/shard_map/all_to_all | solution.py:12
  165.8 3.5 %fusion.59 = f32[8,32,128]{2,1,0:T(8,128)S(1)} fusion(f32[32,8,6,128]{3,0,2,1:T(8,128)S(1)} %bitcast.395, f32[2,8,8,128,128]{4,3,2,1,0:T(8,128)} %param.12), kind=kOutput, calls=%fused_computation.94 | convolution fusion | flops 150994944 | bytes 4063232 | tf_op jit(solution)/shard_map/tbkc,bkrc->tbr/dot_general | solution.py:65
  169.3 6.9 %all-to-all-done.7 = f32[32,32,128]{2,1,0:T(8,128)S(1)} async-done(((f32[32,32,128]{2,1,0:T(8,128)}), f32[32,32,128]{2,1,0:T(8,128)S(1)}, u32[]{:S(2)}, u32[]{:S(2)}) %all-to-all-start.7) | async-done | bytes 524320 | tf_op jit(solution)/shard_map/all_to_all | solution.py:12
  176.8 1.9 fusion.46
  179.5 0.9 pad_maximum_fusion
  180.4 4.1 %all-to-all-start.8 = ((f32[32,40,128]{2,1,0:T(8,128)}), f32[32,40,128]{2,1,0:T(8,128)S(1)}, u32[]{:S(2)}, u32[]{:S(2)}) async-start(f32[32,40,128]{2,1,0:T(8,128)} %pad_maximum_fusion), calls=%async_computation.8 | async-start | bytes 1310720 | tf_op jit(solution)/shard_map/all_to_all | solution.py:12
  185.1 3.5 %fusion.74 = f32[8,32,128]{2,1,0:T(8,128)S(1)} fusion(f32[32,8,6,128]{3,0,2,1:T(8,128)S(1)} %bitcast.396, f32[2,8,8,128,128]{4,3,2,1,0:T(8,128)} %param.12), kind=kOutput, calls=%fused_computation.99 | convolution fusion | flops 150994944 | bytes 4063232 | tf_op jit(solution)/shard_map/tbkc,bkrc->tbr/dot_general | solution.py:65
  188.6 8.4 %all-to-all-done.8 = f32[32,40,128]{2,1,0:T(8,128)S(1)} async-done(((f32[32,40,128]{2,1,0:T(8,128)}), f32[32,40,128]{2,1,0:T(8,128)S(1)}, u32[]{:S(2)}, u32[]{:S(2)}) %all-to-all-start.8) | async-done | bytes 655392 | tf_op jit(solution)/shard_map/all_to_all | solution.py:12
  197.7 1.9 fusion.47
  199.7 7.2 %collective-permute-done.3 = f32[32,1024]{1,0:T(8,128)S(1)} collective-permute-done((f32[32,1024]{1,0:T(8,128)S(1)}, f32[32,1024]{1,0:T(8,128)S(1)}, u32[]{:S(2)}, u32[]{:S(2)}) %collective-permute-start.3) | collective-permute-done | bytes 131104 | tf_op jit(solution)/shard_map/ppermute | solution.py:99
  207.0 1.4 gather_fusion.25
  208.4 4.1 %all-to-all-start.9 = ((f32[32,32,128]{2,1,0:T(8,128)}), f32[32,32,128]{2,1,0:T(8,128)S(1)}, u32[]{:S(2)}, u32[]{:S(2)}) async-start(f32[32,32,128]{2,1,0:T(8,128)} %gather_fusion.25), calls=%async_computation.9 | async-start | bytes 1048576 | tf_op jit(solution)/shard_map/all_to_all | solution.py:12
  213.1 3.5 %fusion.62 = f32[8,32,128]{2,1,0:T(8,128)S(1)} fusion(f32[32,8,6,128]{3,0,2,1:T(8,128)S(1)} %bitcast.388, f32[2,8,8,128,128]{4,3,2,1,0:T(8,128)} %param.12), kind=kOutput, calls=%fused_computation.95 | convolution fusion | flops 150994944 | bytes 4063232 | tf_op jit(solution)/shard_map/tbkc,bkrc->tbr/dot_general | solution.py:65
  216.6 6.7 %all-to-all-done.9 = f32[32,32,128]{2,1,0:T(8,128)S(1)} async-done(((f32[32,32,128]{2,1,0:T(8,128)}), f32[32,32,128]{2,1,0:T(8,128)S(1)}, u32[]{:S(2)}, u32[]{:S(2)}) %all-to-all-start.9) | async-done | bytes 524320 | tf_op jit(solution)/shard_map/all_to_all | solution.py:12
  223.9 1.9 fusion.48
  226.6 0.9 pad_maximum_fusion.1
  227.4 4.1 %all-to-all-start.10 = ((f32[32,40,128]{2,1,0:T(8,128)}), f32[32,40,128]{2,1,0:T(8,128)S(1)}, u32[]{:S(2)}, u32[]{:S(2)}) async-start(f32[32,40,128]{2,1,0:T(8,128)} %pad_maximum_fusion.1), calls=%async_computation.10 | async-start | bytes 1310720 | tf_op jit(solution)/shard_map/all_to_all | solution.py:12
  231.6 1.3 collective-permute-start.6
  232.9 0.7 collective-permute-start.5
  234.2 3.5 %fusion.77 = f32[8,32,128]{2,1,0:T(8,128)S(1)} fusion(f32[32,8,6,128]{3,0,2,1:T(8,128)S(1)} %bitcast.389, f32[2,8,8,128,128]{4,3,2,1,0:T(8,128)} %param.12), kind=kOutput, calls=%fused_computation.100 | convolution fusion | flops 150994944 | bytes 4063232 | tf_op jit(solution)/shard_map/tbkc,bkrc->tbr/dot_general | solution.py:65
  237.7 6.4 %all-to-all-done.10 = f32[32,40,128]{2,1,0:T(8,128)S(1)} async-done(((f32[32,40,128]{2,1,0:T(8,128)}), f32[32,40,128]{2,1,0:T(8,128)S(1)}, u32[]{:S(2)}, u32[]{:S(2)}) %all-to-all-start.10) | async-done | bytes 655392 | tf_op jit(solution)/shard_map/all_to_all | solution.py:12
  244.8 1.8 fusion.49
  246.8 0.7 collective-permute-start.4
  247.5 0.6 slice_select_fusion.2
  (100 shorter events, 17.1 us)
Async XLA Ops:
  0.0 42.5 %copy-start = (f32[64,1024]{1,0:T(8,128)S(1)}, f32[64,1024]{1,0:T(8,128)}, u32[]{:S(2)}) copy-start(f32[64,1024]{1,0:T(8,128)} %param.9) | copy-start | bytes 786436
  0.0 29.1 %copy-start.1 = (f32[2,1024]{1,0:T(2,128)S(1)}, f32[2,1024]{1,0:T(2,128)}, u32[]{:S(2)}) copy-start(f32[2,1024]{1,0:T(2,128)} %param.11) | copy-start | bytes 24580
  3.6 16.2 %all-to-all-start = ((f32[32,1,130]{2,1,0:T(1,128)}), f32[32,1,130]{2,1,0:T(1,128)S(1)}, u32[]{:S(2)}, u32[]{:S(2)}) async-start(f32[32,1,130]{2,1,0:T(1,128)} %all_to_all.38), calls=%async_computation | async-start | bytes 65536 | tf_op jit(solution)/shard_map/all_to_all | solution.py:12
  21.6 18.5 %all-to-all-start.1 = ((f32[32,32,128]{2,1,0:T(8,128)}), f32[32,32,128]{2,1,0:T(8,128)S(1)}, u32[]{:S(2)}, u32[]{:S(2)}) async-start(f32[32,32,128]{2,1,0:T(8,128)} %gather_fusion.1), calls=%async_computation.1 | async-start | bytes 1048576 | tf_op jit(solution)/shard_map/all_to_all | solution.py:12
  43.9 15.2 %all-to-all-start.2 = ((f32[32,32,128]{2,1,0:T(8,128)}), f32[32,32,128]{2,1,0:T(8,128)S(1)}, u32[]{:S(2)}, u32[]{:S(2)}) async-start(f32[32,32,128]{2,1,0:T(8,128)} %gather_fusion.4), calls=%async_computation.2 | async-start | bytes 1048576 | tf_op jit(solution)/shard_map/all_to_all | solution.py:12
  61.6 7.5 %collective-permute-start = (f32[32,1024]{1,0:T(8,128)S(1)}, f32[32,1024]{1,0:T(8,128)S(1)}, u32[]{:S(2)}, u32[]{:S(2)}) collective-permute-start(f32[32,1024]{1,0:T(8,128)S(1)} %bitcast_add_fusion.8), channel_id=1, source_target_pairs={{0,32},{32,64},{64,96},{96,0},{1,33},{33,65},{65,97},{97,1},{2,34}... | collective-permute-start | bytes 393224 | tf_op jit(solution)/shard_map/ppermute | solution.py:99
  70.4 15.0 %all-to-all-start.3 = ((f32[32,32,128]{2,1,0:T(8,128)}), f32[32,32,128]{2,1,0:T(8,128)S(1)}, u32[]{:S(2)}, u32[]{:S(2)}) async-start(f32[32,32,128]{2,1,0:T(8,128)} %gather_fusion.7), calls=%async_computation.3 | async-start | bytes 1048576 | tf_op jit(solution)/shard_map/all_to_all | solution.py:12
  89.3 15.2 %all-to-all-start.4 = ((f32[32,32,128]{2,1,0:T(8,128)}), f32[32,32,128]{2,1,0:T(8,128)S(1)}, u32[]{:S(2)}, u32[]{:S(2)}) async-start(f32[32,32,128]{2,1,0:T(8,128)} %gather_fusion.10), calls=%async_computation.4 | async-start | bytes 1048576 | tf_op jit(solution)/shard_map/all_to_all | solution.py:12
  106.9 7.5 %collective-permute-start.1 = (f32[32,1024]{1,0:T(8,128)S(1)}, f32[32,1024]{1,0:T(8,128)S(1)}, u32[]{:S(2)}, u32[]{:S(2)}) collective-permute-start(f32[32,1024]{1,0:T(8,128)S(1)} %bitcast_add_fusion.6), channel_id=1, source_target_pairs={{0,32},{32,64},{64,96},{96,0},{1,33},{33,65},{65,97},{97,1},{2,34}... | collective-permute-start | bytes 393224 | tf_op jit(solution)/shard_map/ppermute | solution.py:99
  115.8 15.1 %all-to-all-start.5 = ((f32[32,32,128]{2,1,0:T(8,128)}), f32[32,32,128]{2,1,0:T(8,128)S(1)}, u32[]{:S(2)}, u32[]{:S(2)}) async-start(f32[32,32,128]{2,1,0:T(8,128)} %gather_fusion.13), calls=%async_computation.5 | async-start | bytes 1048576 | tf_op jit(solution)/shard_map/all_to_all | solution.py:12
  134.8 15.2 %all-to-all-start.6 = ((f32[32,32,128]{2,1,0:T(8,128)}), f32[32,32,128]{2,1,0:T(8,128)S(1)}, u32[]{:S(2)}, u32[]{:S(2)}) async-start(f32[32,32,128]{2,1,0:T(8,128)} %gather_fusion.16), calls=%async_computation.6 | async-start | bytes 1048576 | tf_op jit(solution)/shard_map/all_to_all | solution.py:12
  152.4 7.5 %collective-permute-start.2 = (f32[32,1024]{1,0:T(8,128)S(1)}, f32[32,1024]{1,0:T(8,128)S(1)}, u32[]{:S(2)}, u32[]{:S(2)}) collective-permute-start(f32[32,1024]{1,0:T(8,128)S(1)} %bitcast_add_fusion.4), channel_id=1, source_target_pairs={{0,32},{32,64},{64,96},{96,0},{1,33},{33,65},{65,97},{97,1},{2,34}... | collective-permute-start | bytes 393224 | tf_op jit(solution)/shard_map/ppermute | solution.py:99
  161.3 15.0 %all-to-all-start.7 = ((f32[32,32,128]{2,1,0:T(8,128)}), f32[32,32,128]{2,1,0:T(8,128)S(1)}, u32[]{:S(2)}, u32[]{:S(2)}) async-start(f32[32,32,128]{2,1,0:T(8,128)} %gather_fusion.19), calls=%async_computation.7 | async-start | bytes 1048576 | tf_op jit(solution)/shard_map/all_to_all | solution.py:12
  165.8 31.9 %copy-start.2 = (f32[64]{0:T(128)S(1)}, f32[64]{0:T(128)}, u32[]{:S(2)}) copy-start(f32[64]{0:T(128)} %param.10) | copy-start | bytes 772
  180.4 16.6 %all-to-all-start.8 = ((f32[32,40,128]{2,1,0:T(8,128)}), f32[32,40,128]{2,1,0:T(8,128)S(1)}, u32[]{:S(2)}, u32[]{:S(2)}) async-start(f32[32,40,128]{2,1,0:T(8,128)} %pad_maximum_fusion), calls=%async_computation.8 | async-start | bytes 1310720 | tf_op jit(solution)/shard_map/all_to_all | solution.py:12
  199.7 7.3 %collective-permute-start.3 = (f32[32,1024]{1,0:T(8,128)S(1)}, f32[32,1024]{1,0:T(8,128)S(1)}, u32[]{:S(2)}, u32[]{:S(2)}) collective-permute-start(f32[32,1024]{1,0:T(8,128)S(1)} %get-tuple-element.32), channel_id=1, source_target_pairs={{0,32},{32,64},{64,96},{96,0},{1,33},{33,65},{65,97},{97,1},{2,34}... | collective-permute-start | bytes 393224 | tf_op jit(solution)/shard_map/ppermute | solution.py:99
  208.4 15.0 %all-to-all-start.9 = ((f32[32,32,128]{2,1,0:T(8,128)}), f32[32,32,128]{2,1,0:T(8,128)S(1)}, u32[]{:S(2)}, u32[]{:S(2)}) async-start(f32[32,32,128]{2,1,0:T(8,128)} %gather_fusion.25), calls=%async_computation.9 | async-start | bytes 1048576 | tf_op jit(solution)/shard_map/all_to_all | solution.py:12
  227.4 16.6 %all-to-all-start.10 = ((f32[32,40,128]{2,1,0:T(8,128)}), f32[32,40,128]{2,1,0:T(8,128)S(1)}, u32[]{:S(2)}, u32[]{:S(2)}) async-start(f32[32,40,128]{2,1,0:T(8,128)} %pad_maximum_fusion.1), calls=%async_computation.10 | async-start | bytes 1310720 | tf_op jit(solution)/shard_map/all_to_all | solution.py:12
  231.6 15.9 %collective-permute-start.6 = (f32[16,1024]{1,0:T(8,128)S(1)}, f32[16,1024]{1,0:T(8,128)S(1)}, u32[]{:S(2)}, u32[]{:S(2)}) collective-permute-start(f32[16,1024]{1,0:T(8,128)S(1)} %get-tuple-element.37), channel_id=1, source_target_pairs={{96,0},{97,1},{98,2},{99,3},{100,4},{101,5},{102,6},{103,7},{104,8... | collective-permute-start | bytes 196616 | tf_op jit(solution)/shard_map/ppermute | solution.py:96
  232.9 14.6 %collective-permute-start.5 = (f32[16,1024]{1,0:T(8,128)S(1)}, f32[16,1024]{1,0:T(8,128)S(1)}, u32[]{:S(2)}, u32[]{:S(2)}) collective-permute-start(f32[16,1024]{1,0:T(8,128)S(1)} %get-tuple-element.38), channel_id=1, source_target_pairs={{96,32},{97,33},{98,34},{99,35},{100,36},{101,37},{102,38},{103,39... | collective-permute-start | bytes 196616 | tf_op jit(solution)/shard_map/ppermute | solution.py:96
  246.8 0.7 collective-permute-start.4
